TPU v7x, 128 devices: a whole 4x4x4 slice. The times are simulated.
128 devices in a mesh: row: 4 (over z_lo, core), col: 4 (over x), slab: 8 (over y, z_hi).
Axes of the slice: x: 4, y: 4, z: 4 (z_hi: 2, z_lo: 2; z = z_hi * 2 + z_lo), core: 2. Of those that a mesh axis runs over, the one named last changes fastest.
Arguments:
- amplitudes: bfloat16 [48, 48, 480, 128], P('row', 'col', 'slab'), may hold values from -6 to 6
- integrals: bfloat16 [48, 480, 48, 128], P('row', 'slab', 'col'), may hold values from -0.0625 to 0.0625
- irreps: int32 [19], replicated, may hold values from 0 to 1
- pair_mask: int32 [4, 4], replicated, may hold values 0 or 1
Outputs:
- cycle_term: bfloat16 [48, 48, 128, 128], P('row', 'col', 'slab')
Inputs may be any that keep to these rules, and one draw needn't show every extreme that they name: Each label is one of the two irreps of the point group. `pair_mask`: 1 marks a block pair whose amplitudes are kept.
All inputs are finite; a program needn't handle non-finite values.
Results may differ from a plain program's by a relative error of at most 0.001.
Values may be sent and summed in bfloat16 or wider, within the bound.
No kernel may reach another device: no remote copies, remote signals or barrier semaphores. Data moves between devices by JAX's collectives and lax.ppermute only.
A program may use at most 128 MiB of HBM per device.

v0:
```python
import jax
import jax.numpy as jnp
from jax import lax
from jax.sharding import PartitionSpec as P

OBLK = 12
VTILE = 32


def shifted(value, axis, fn):
    size = lax.axis_size(axis)
    return lax.ppermute(value, axis, [(src, fn(src) % size) for src in range(size)])


def int_mask(irreps, blocks, row_at, col_at, slab_at, c_cols, win_cols):
    c_ids = slab_at * c_cols + jnp.arange(c_cols, dtype=jnp.int32)
    b_ids = jnp.arange(win_cols, dtype=jnp.int32)
    label_c = jnp.take(irreps, blocks + c_ids // VTILE)
    label_b = jnp.take(irreps, blocks + b_ids // VTILE)
    occ = irreps[row_at] + irreps[col_at]
    parity = occ + label_c[:, None] + label_b[None, :]
    return parity % 2 == 0


def gather_row(ints, row_at):
    zpart = shifted(ints, "row", lambda r: r ^ 2)
    blocks = [ints, shifted(ints, "row", lambda r: r ^ 1), zpart, shifted(zpart, "row", lambda r: r ^ 1)]
    k_rows = ints.shape[0]
    whole = jnp.zeros((len(blocks) * k_rows,) + ints.shape[1:], ints.dtype)
    for u, blk in enumerate(blocks):
        whole = lax.dynamic_update_slice_in_dim(whole, blk, (row_at ^ u) * k_rows, axis=0)
    return whole


def ring_reduce_y(part, slab_at, split_axis):
    ny = lax.axis_size("slab") // 2
    width = part.shape[2] // ny
    y_at = slab_at // 2
    half = part.shape[split_axis] // 2
    halves = tuple(lax.slice_in_dim(part, h * half, (h + 1) * half, axis=split_axis) for h in range(2))
    dirs = (1, -1)
    acc = [None, None]
    for step in range(ny - 1):
        for h in range(2):
            d = dirs[h]
            chunk = (y_at - d * (step + 1)) % ny
            own = lax.dynamic_slice_in_dim(halves[h], chunk * width, width, axis=2)
            send = own if acc[h] is None else acc[h] + own
            acc[h] = shifted(send, "slab", lambda s, d=d: s + 2 * d)
    result = []
    for h in range(2):
        own = lax.dynamic_slice_in_dim(halves[h], y_at * width, width, axis=2)
        result.append(acc[h] + own)
    return jnp.concatenate(result, axis=split_axis)


def body(amplitudes, integrals, irreps, pair_mask):
    i_rows, k_rows, c_cols, win_cols = amplitudes.shape
    blocks = pair_mask.shape[0]
    row_at = lax.axis_index("row")
    col_at = lax.axis_index("col")
    slab_at = lax.axis_index("slab")
    n_slab = lax.axis_size("slab")

    keep = pair_mask[row_at, col_at] != 0
    amp = jnp.where(keep, amplitudes, jnp.zeros_like(amplitudes))
    mask = int_mask(irreps, blocks, row_at, col_at, slab_at, c_cols, win_cols)
    ints = jnp.where(mask[None, :, None, :], integrals, jnp.zeros_like(integrals))

    amp_all = lax.all_gather(amp, "col", axis=1, tiled=True)
    int_abs = gather_row(ints, row_at)
    n_row = lax.axis_size("row")
    n_col = lax.axis_size("col")
    n_chunks = 2
    rows = i_rows // n_chunks
    share_parts = []
    for ch in range(n_chunks):
        amp_part = lax.slice_in_dim(amp_all, ch * rows, (ch + 1) * rows, axis=0)
        part = jnp.einsum("ikca,kcjb->ijab", amp_part, int_abs, preferred_element_type=jnp.float32)
        reduced_y = ring_reduce_y(part, slab_at, 1)
        zh = slab_at % 2
        width = reduced_y.shape[2] // 2
        mine = lax.dynamic_slice_in_dim(reduced_y, zh * width, width, axis=2)
        theirs = lax.dynamic_slice_in_dim(reduced_y, (1 - zh) * width, width, axis=2)
        shares = mine + shifted(theirs, "slab", lambda s: s ^ 1)
        share_parts.append(shares)
    shares = jnp.concatenate(share_parts, axis=0)

    i_n, j_n, a_n, b_n = shares.shape
    outgoing = jnp.transpose(shares.reshape(i_n, j_n, a_n, n_slab, b_n // n_slab), (3, 1, 0, 4, 2))
    outgoing = outgoing.reshape(n_slab, j_n * i_n, a_n * a_n)
    gathered = jnp.zeros((n_slab, j_n * i_n, a_n * a_n), shares.dtype)
    for d in range(n_slab):
        flat = lax.dynamic_slice_in_dim(outgoing, slab_at ^ d, 1, axis=0)
        pairs = [
            ((r * n_col + c) * n_slab + t, (c * n_col + r) * n_slab + (t ^ d))
            for r in range(n_row)
            for c in range(n_col)
            for t in range(n_slab)
        ]
        flat = lax.ppermute(flat, ("row", "col", "slab"), pairs)
        gathered = lax.dynamic_update_slice_in_dim(gathered, flat, slab_at ^ d, axis=0)
    gathered = gathered.reshape(n_slab, j_n, i_n, a_n, a_n)
    mirrored = jnp.transpose(gathered, (1, 2, 3, 0, 4)).reshape(shares.shape)
    return (shares + mirrored).astype(jnp.bfloat16)


def solution(mesh):
    return jax.shard_map(
        body,
        mesh=mesh,
        in_specs=(P("row", "col", "slab", None), P("row", "slab", "col", None), P(), P()),
        out_specs=P("row", "col", "slab", None),
        check_vma=False,
    )
```

profile of v0, /device:TPU:0, one launch (start us, length us, event | category | flops | bytes accessed | tf_op | source)
XLA Modules:
  0.0 317.7 jit_solution(11527965652140456381)
XLA Ops:
  15.7 11.8 %and_select_fusion.1 = s32[128]{0:T(128)S(1)} fusion(s32[]{:T(128)} %bitcast.26, s32[]{:T(128)} %bitcast.27, s32[]{:T(128)} %bitcast.28, s32[]{:T(128)} %bitcast.29, s32[]{:T(128)} %bitcast.30, s32[]{:T(128)} %bitcast.32, s32[]{:T(128)} %bitcast.31, s32[]{:T(128)} %bitcast.3, s32[]{:T(128)} %bitcast.5, s32[]{:T(128)} %bitcast.7, s32[]{:T(128)} %bitcast.9, ...), kind=kLoop, calls=%fused_computation.94 | loop fusion | flops 8192 | bytes 588 | tf_op jit(solution)/shard_map/jit(_take)/select_n | solution.py:19
  30.8 52.0 %collective-permute-done.1 = bf16[12,60,12,128]{3,1,2,0:T(8,128)(2,1)} collective-permute-done((bf16[12,60,12,128]{3,1,2,0:T(8,128)(2,1)}, bf16[12,60,12,128]{3,1,2,0:T(8,128)(2,1)}, u32[]{:S(2)}, u32[]{:S(2)}) %collective-permute-start.1) | collective-permute-done | bytes 2211872 | tf_op jit(solution)/shard_map/ppermute | solution.py:12
  82.8 6.0 %broadcast_in_dim.35 = bf16[48,60,12,128]{3,1,0,2:T(8,128)(2,1)} broadcast(bf16[]{:T(256)} %constant.161.clone.1), dimensions={} | broadcast | bytes 8847362 | tf_op jit(solution)/shard_map/broadcast_in_dim | solution.py:29
  91.0 3.8 %copy_dynamic-update-slice_fusion.2 = bf16[48,60,12,128]{3,1,0,2:T(8,128)(2,1)} fusion(bf16[48,60,12,128]{3,1,0,2:T(8,128)(2,1)} %copy_dynamic-update-slice_fusion.3, s32[]{:T(128)S(6)} %select_n.273, bf16[12,60,12,128]{3,1,2,0:T(8,128)(2,1)} %collective-permute-done), kind=kLoop, calls=%fused_computation.9 | loop fusion | bytes 4718596 | tf_op jit(solution)/shard_map/dynamic_update_slice | solution.py:31
  94.8 3.8 %copy_dynamic-update-slice_fusion.1 = bf16[48,60,12,128]{3,1,0,2:T(8,128)(2,1)} fusion(bf16[48,60,12,128]{3,1,0,2:T(8,128)(2,1)} %copy_dynamic-update-slice_fusion.2, s32[]{:T(128)S(6)} %select_n.274, bf16[12,60,12,128]{3,1,2,0:T(8,128)(2,1)} %collective-permute-done.1), kind=kLoop, calls=%fused_computation.8 | loop fusion | bytes 4718596 | tf_op jit(solution)/shard_map/dynamic_update_slice | solution.py:31
  98.6 3.8 %copy_dynamic-update-slice_fusion = bf16[48,60,12,128]{3,1,0,2:T(8,128)(2,1)} fusion(bf16[48,60,12,128]{3,1,0,2:T(8,128)(2,1)} %copy_dynamic-update-slice_fusion.1, s32[]{:T(128)S(6)} %select_n.275, bf16[12,60,12,128]{3,1,2,0:T(8,128)(2,1)} %collective-permute-done.2), kind=kLoop, calls=%fused_computation.7 | loop fusion | bytes 4718596 | tf_op jit(solution)/shard_map/dynamic_update_slice | solution.py:31
  102.3 3.8 %all-gather.2.cloned.1.call-done = bf16[12,48,60,128]{3,2,1,0:T(8,128)(2,1)} async-done(((bf16[12,12,60,128]{3,2,1,0:T(8,128)(2,1)}), bf16[12,48,60,128]{3,2,1,0:T(8,128)(2,1)}) %all-gather.2.cloned.1.call-update) | async-done | bytes 8847376 | tf_op jit(solution)/shard_map/all_gather | solution.py:70
  106.1 11.6 %fusion.4 = f32[6,12,128,128]{3,2,0,1:T(8,128)S(1)} fusion(bf16[12,48,60,128]{3,2,1,0:T(8,128)(2,1)} %all-gather.2.cloned.1.call-done, bf16[48,60,12,128]{3,1,0,2:T(8,128)(2,1)} %copy_dynamic-update-slice_fusion), kind=kOutput, calls=%fused_computation.13 | convolution fusion | flops 6794772480 | bytes 18874368 | tf_op jit(solution)/shard_map/ikca,kcjb->ijab/dot_general | solution.py:79
  121.5 10.1 %fusion.7 = f32[6,12,128,128]{3,2,0,1:T(8,128)S(1)} fusion(bf16[12,48,60,128]{3,2,1,0:T(8,128)(2,1)S(1)} %copy-done.2, bf16[48,60,12,128]{3,1,0,2:T(8,128)(2,1)} %copy_dynamic-update-slice_fusion), kind=kOutput, calls=%fused_computation.14 | convolution fusion | flops 6794772480 | bytes 18284544 | tf_op jit(solution)/shard_map/ikca,kcjb->ijab/dot_general | solution.py:79
  132.3 3.3 %collective-permute-start.13 = (f32[6,6,32,128]{3,2,0,1:T(8,128)S(1)}, f32[6,6,32,128]{3,2,0,1:T(8,128)S(1)}, u32[]{:S(2)}, u32[]{:S(2)}) collective-permute-start(f32[6,6,32,128]{3,2,0,1:T(8,128)S(1)} %constant_dynamic-slice_fusion.8), channel_id=1, source_target_pairs={{0,6},{1,7},{2,0},{3,1},{4,2},{5,3},{6,4},{7,5},{8,14},{9,15},{10,... | collective-permute-start | bytes 1769480 | tf_op jit(solution)/shard_map/ppermute | solution.py:12
  135.8 3.3 %collective-permute-start.7 = (f32[6,6,32,128]{3,2,0,1:T(8,128)S(1)}, f32[6,6,32,128]{3,2,0,1:T(8,128)S(1)}, u32[]{:S(2)}, u32[]{:S(2)}) collective-permute-start(f32[6,6,32,128]{3,2,0,1:T(8,128)S(1)} %dynamic-slice_add_fusion.8), channel_id=1, source_target_pairs={{0,6},{1,7},{2,0},{3,1},{4,2},{5,3},{6,4},{7,5},{8,14},{9,15},{10,... | collective-permute-start | bytes 1769480 | tf_op jit(solution)/shard_map/ppermute | solution.py:12
  139.3 10.0 %collective-permute-done.13 = f32[6,6,32,128]{3,2,0,1:T(8,128)S(1)} collective-permute-done((f32[6,6,32,128]{3,2,0,1:T(8,128)S(1)}, f32[6,6,32,128]{3,2,0,1:T(8,128)S(1)}, u32[]{:S(2)}, u32[]{:S(2)}) %collective-permute-start.13) | collective-permute-done | bytes 589856 | tf_op jit(solution)/shard_map/ppermute | solution.py:12
  149.4 3.8 %collective-permute-start.14 = (f32[6,6,32,128]{3,2,0,1:T(8,128)S(1)}, f32[6,6,32,128]{3,2,0,1:T(8,128)S(1)}, u32[]{:S(2)}, u32[]{:S(2)}) collective-permute-start(f32[6,6,32,128]{3,2,0,1:T(8,128)S(1)} %dynamic-slice_add_fusion.2), channel_id=1, source_target_pairs={{0,6},{1,7},{2,0},{3,1},{4,2},{5,3},{6,4},{7,5},{8,14},{9,15},{10,... | collective-permute-start | bytes 1769480 | tf_op jit(solution)/shard_map/ppermute | solution.py:12
  153.3 8.6 %collective-permute-done.7 = f32[6,6,32,128]{3,2,0,1:T(8,128)S(1)} collective-permute-done((f32[6,6,32,128]{3,2,0,1:T(8,128)S(1)}, f32[6,6,32,128]{3,2,0,1:T(8,128)S(1)}, u32[]{:S(2)}, u32[]{:S(2)}) %collective-permute-start.7) | collective-permute-done | bytes 589856 | tf_op jit(solution)/shard_map/ppermute | solution.py:12
  162.0 3.8 %collective-permute-start.8 = (f32[6,6,32,128]{3,2,0,1:T(8,128)S(1)}, f32[6,6,32,128]{3,2,0,1:T(8,128)S(1)}, u32[]{:S(2)}, u32[]{:S(2)}) collective-permute-start(f32[6,6,32,128]{3,2,0,1:T(8,128)S(1)} %dynamic-slice_add_fusion.7), channel_id=1, source_target_pairs={{0,6},{1,7},{2,0},{3,1},{4,2},{5,3},{6,4},{7,5},{8,14},{9,15},{10,... | collective-permute-start | bytes 1769480 | tf_op jit(solution)/shard_map/ppermute | solution.py:12
  166.0 8.6 %collective-permute-done.14 = f32[6,6,32,128]{3,2,0,1:T(8,128)S(1)} collective-permute-done((f32[6,6,32,128]{3,2,0,1:T(8,128)S(1)}, f32[6,6,32,128]{3,2,0,1:T(8,128)S(1)}, u32[]{:S(2)}, u32[]{:S(2)}) %collective-permute-start.14) | collective-permute-done | bytes 589856 | tf_op jit(solution)/shard_map/ppermute | solution.py:12
  174.7 3.8 %collective-permute-start.15 = (f32[6,6,32,128]{3,2,0,1:T(8,128)S(1)}, f32[6,6,32,128]{3,2,0,1:T(8,128)S(1)}, u32[]{:S(2)}, u32[]{:S(2)}) collective-permute-start(f32[6,6,32,128]{3,2,0,1:T(8,128)S(1)} %dynamic-slice_add_fusion.1), channel_id=1, source_target_pairs={{0,6},{1,7},{2,0},{3,1},{4,2},{5,3},{6,4},{7,5},{8,14},{9,15},{10,... | collective-permute-start | bytes 1769480 | tf_op jit(solution)/shard_map/ppermute | solution.py:12
  178.6 8.6 %collective-permute-done.8 = f32[6,6,32,128]{3,2,0,1:T(8,128)S(1)} collective-permute-done((f32[6,6,32,128]{3,2,0,1:T(8,128)S(1)}, f32[6,6,32,128]{3,2,0,1:T(8,128)S(1)}, u32[]{:S(2)}, u32[]{:S(2)}) %collective-permute-start.8) | collective-permute-done | bytes 589856 | tf_op jit(solution)/shard_map/ppermute | solution.py:12
  187.3 3.7 %collective-permute-done.5 = f32[6,6,32,128]{3,2,0,1:T(8,128)S(1)} collective-permute-done((f32[6,6,32,128]{3,2,0,1:T(8,128)S(1)}, f32[6,6,32,128]{3,2,0,1:T(8,128)S(1)}, u32[]{:S(2)}, u32[]{:S(2)}) %collective-permute-start.5) | collective-permute-done | bytes 589856 | tf_op jit(solution)/shard_map/ppermute | solution.py:12
  194.4 3.6 %collective-permute-done.15 = f32[6,6,32,128]{3,2,0,1:T(8,128)S(1)} collective-permute-done((f32[6,6,32,128]{3,2,0,1:T(8,128)S(1)}, f32[6,6,32,128]{3,2,0,1:T(8,128)S(1)}, u32[]{:S(2)}, u32[]{:S(2)}) %collective-permute-start.15) | collective-permute-done | bytes 589856 | tf_op jit(solution)/shard_map/ppermute | solution.py:12
  198.1 3.4 %collective-permute-done.12 = f32[6,6,32,128]{3,2,0,1:T(8,128)S(1)} collective-permute-done((f32[6,6,32,128]{3,2,0,1:T(8,128)S(1)}, f32[6,6,32,128]{3,2,0,1:T(8,128)S(1)}, u32[]{:S(2)}, u32[]{:S(2)}) %collective-permute-start.12) | collective-permute-done | bytes 589856 | tf_op jit(solution)/shard_map/ppermute | solution.py:12
  205.7 11.8 %collective-permute-done.16 = f32[6,12,16,128]{3,2,0,1:T(8,128)} collective-permute-done((f32[6,12,16,128]{3,2,0,1:T(8,128)}, f32[6,12,16,128]{3,2,0,1:T(8,128)}, u32[]{:S(2)}, u32[]{:S(2)}) %collective-permute-start.16) | collective-permute-done | bytes 589856 | tf_op jit(solution)/shard_map/ppermute | solution.py:12
  218.8 5.0 %reshape.206 = f32[12,12,16,8,16]{4,3,2,0,1:T(8,128)} reshape(f32[12,12,16,128]{3,2,0,1:T(8,128)S(1)} %pad_maximum_fusion) | data formatting | bytes 2359296 | tf_op jit(solution)/shard_map/reshape | solution.py:90
  223.8 9.6 %copy.14 = f32[12,12,16,8,16]{2,4,0,1,3:T(8,128)} copy(f32[12,12,16,8,16]{4,3,2,0,1:T(8,128)} %reshape.206) | data formatting | bytes 2359296 | tf_op jit(solution)/shard_map/reshape | solution.py:90
  233.4 6.9 %reshape.207 = f32[8,144,256]{2,1,0:T(8,128)S(1)} reshape(f32[8,12,12,16,16]{4,3,2,1,0:T(8,128)} %bitcast.142) | data formatting | bytes 2359296 | tf_op jit(solution)/shard_map/reshape | solution.py:91
  246.3 5.9 %collective-permute-start.22 = (f32[1,144,256]{2,1,0:T(8,128)S(1)}, f32[1,144,256]{2,1,0:T(8,128)S(1)}, u32[]{:S(2)}, u32[]{:S(2)}) collective-permute-start(f32[1,144,256]{2,1,0:T(8,128)S(1)} %get-tuple-element.11), channel_id=1, source_target_pairs={{0,5},{1,4},{2,7},{3,6},{4,1},{5,0},{6,3},{7,2},{8,37},{9,36},{10,... | collective-permute-start | bytes 442376 | tf_op jit(solution)/shard_map/ppermute | solution.py:101
  254.5 7.3 %collective-permute-start.24 = (f32[1,144,256]{2,1,0:T(8,128)S(1)}, f32[1,144,256]{2,1,0:T(8,128)S(1)}, u32[]{:S(2)}, u32[]{:S(2)}) collective-permute-start(f32[1,144,256]{2,1,0:T(8,128)S(1)} %get-tuple-element.9), channel_id=1, source_target_pairs={{0,7},{1,6},{2,5},{3,4},{4,3},{5,2},{6,1},{7,0},{8,39},{9,38},{10,... | collective-permute-start | bytes 442376 | tf_op jit(solution)/shard_map/ppermute | solution.py:101
  261.8 17.8 %collective-permute-done.21 = f32[1,144,256]{2,1,0:T(8,128)S(1)} collective-permute-done((f32[1,144,256]{2,1,0:T(8,128)S(1)}, f32[1,144,256]{2,1,0:T(8,128)S(1)}, u32[]{:S(2)}, u32[]{:S(2)}) %collective-permute-start.21) | collective-permute-done | bytes 147488 | tf_op jit(solution)/shard_map/ppermute | solution.py:101
  279.6 3.8 %collective-permute-done.22 = f32[1,144,256]{2,1,0:T(8,128)S(1)} collective-permute-done((f32[1,144,256]{2,1,0:T(8,128)S(1)}, f32[1,144,256]{2,1,0:T(8,128)S(1)}, u32[]{:S(2)}, u32[]{:S(2)}) %collective-permute-start.22) | collective-permute-done | bytes 147488 | tf_op jit(solution)/shard_map/ppermute | solution.py:101
  285.6 5.1 %reshape.208 = f32[8,12,12,16,16]{4,3,2,1,0:T(8,128)} reshape(f32[8,144,256]{2,1,0:T(8,128)S(1)} %constant_dynamic-update-slice_fusion) | data formatting | bytes 2359296 | tf_op jit(solution)/shard_map/reshape | solution.py:103
  290.8 12.8 %copy.15 = f32[12,12,16,8,16]{4,3,2,0,1:T(8,128)} copy(f32[12,12,16,8,16]{4,2,1,0,3:T(8,128)} %bitcast.143) | data formatting | bytes 2359296 | tf_op jit(solution)/shard_map/transpose | solution.py:104
  303.5 6.2 %reshape.209 = f32[12,12,16,128]{3,2,0,1:T(8,128)S(1)} reshape(f32[12,12,16,8,16]{4,3,2,0,1:T(8,128)} %copy.15) | data formatting | bytes 2359296 | tf_op jit(solution)/shard_map/reshape | solution.py:104
  (86 shorter events, 38.8 us)
Async XLA Ops:
  6.5 99.6 %all-gather.2.cloned.1.call-start = ((), (), s32[]{:S(2)}) async-start(), calls=%async_computation | async-start | bytes 11796480 | tf_op jit(solution)/shard_map/all_gather | solution.py:70
  11.7 0.7 copy-start
  11.7 16.0 %copy-start.1 = (bf16[12,60,12,128]{3,1,2,0:T(8,128)(2,1)S(1)}, bf16[12,60,12,128]{3,1,2,0:T(8,128)(2,1)}, u32[]{:S(2)}) copy-start(bf16[12,60,12,128]{3,1,2,0:T(8,128)(2,1)} %param.5) | copy-start | bytes 6635524
  29.3 53.6 %collective-permute-start.1 = (bf16[12,60,12,128]{3,1,2,0:T(8,128)(2,1)}, bf16[12,60,12,128]{3,1,2,0:T(8,128)(2,1)}, u32[]{:S(2)}, u32[]{:S(2)}) collective-permute-start(bf16[12,60,12,128]{3,1,2,0:T(8,128)(2,1)} %broadcast_select_fusion.1), channel_id=1, source_target_pairs={{0,64},{32,96},{64,0},{96,32},{1,65},{33,97},{65,1},{97,33},{2,66}... | collective-permute-start | bytes 6635528 | tf_op jit(solution)/shard_map/ppermute | solution.py:12
  29.6 61.3 %collective-permute-start = (bf16[12,60,12,128]{3,1,2,0:T(8,128)(2,1)}, bf16[12,60,12,128]{3,1,2,0:T(8,128)(2,1)}, u32[]{:S(2)}, u32[]{:S(2)}) collective-permute-start(bf16[12,60,12,128]{3,1,2,0:T(8,128)(2,1)} %broadcast_select_fusion.1), channel_id=1, source_target_pairs={{0,32},{32,0},{64,96},{96,64},{1,33},{33,1},{65,97},{97,65},{2,34}... | collective-permute-start | bytes 6635528 | tf_op jit(solution)/shard_map/ppermute | solution.py:12
  82.8 15.7 %collective-permute-start.2 = (bf16[12,60,12,128]{3,1,2,0:T(8,128)(2,1)}, bf16[12,60,12,128]{3,1,2,0:T(8,128)(2,1)}, u32[]{:S(2)}, u32[]{:S(2)}) collective-permute-start(bf16[12,60,12,128]{3,1,2,0:T(8,128)(2,1)} %collective-permute-done.1), channel_id=1, source_target_pairs={{0,32},{32,0},{64,96},{96,64},{1,33},{33,1},{65,97},{97,65},{2,34}... | collective-permute-start | bytes 6635528 | tf_op jit(solution)/shard_map/ppermute | solution.py:12
  117.7 3.7 %copy-start.2 = (bf16[12,48,60,128]{3,2,1,0:T(8,128)(2,1)S(1)}, bf16[12,48,60,128]{3,2,1,0:T(8,128)(2,1)}, u32[]{:S(2)}) copy-start(bf16[12,48,60,128]{3,2,1,0:T(8,128)(2,1)} %all-gather.2.cloned.1.call-done) | copy-start | bytes 26542084
  118.4 17.3 %collective-permute-start.6 = (f32[6,6,32,128]{3,2,0,1:T(8,128)S(1)}, f32[6,6,32,128]{3,2,0,1:T(8,128)S(1)}, u32[]{:S(2)}, u32[]{:S(2)}) collective-permute-start(f32[6,6,32,128]{3,2,0,1:T(8,128)S(1)} %constant_dynamic-slice_fusion.10), channel_id=1, source_target_pairs={{0,6},{1,7},{2,0},{3,1},{4,2},{5,3},{6,4},{7,5},{8,14},{9,15},{10,... | collective-permute-start | bytes 1769480 | tf_op jit(solution)/shard_map/ppermute | solution.py:12
  121.2 17.9 %collective-permute-start.3 = (f32[6,6,32,128]{3,2,0,1:T(8,128)S(1)}, f32[6,6,32,128]{3,2,0,1:T(8,128)S(1)}, u32[]{:S(2)}, u32[]{:S(2)}) collective-permute-start(f32[6,6,32,128]{3,2,0,1:T(8,128)S(1)} %constant_dynamic-slice_fusion.11), channel_id=1, source_target_pairs={{0,2},{1,3},{2,4},{3,5},{4,6},{5,7},{6,0},{7,1},{8,10},{9,11},{10,... | collective-permute-start | bytes 1769480 | tf_op jit(solution)/shard_map/ppermute | solution.py:12
  132.3 17.0 %collective-permute-start.13 = (f32[6,6,32,128]{3,2,0,1:T(8,128)S(1)}, f32[6,6,32,128]{3,2,0,1:T(8,128)S(1)}, u32[]{:S(2)}, u32[]{:S(2)}) collective-permute-start(f32[6,6,32,128]{3,2,0,1:T(8,128)S(1)} %constant_dynamic-slice_fusion.8), channel_id=1, source_target_pairs={{0,6},{1,7},{2,0},{3,1},{4,2},{5,3},{6,4},{7,5},{8,14},{9,15},{10,... | collective-permute-start | bytes 1769480 | tf_op jit(solution)/shard_map/ppermute | solution.py:12
  135.6 17.5 %collective-permute-start.10 = (f32[6,6,32,128]{3,2,0,1:T(8,128)S(1)}, f32[6,6,32,128]{3,2,0,1:T(8,128)S(1)}, u32[]{:S(2)}, u32[]{:S(2)}) collective-permute-start(f32[6,6,32,128]{3,2,0,1:T(8,128)S(1)} %constant_dynamic-slice_fusion.9), channel_id=1, source_target_pairs={{0,2},{1,3},{2,4},{3,5},{4,6},{5,7},{6,0},{7,1},{8,10},{9,11},{10,... | collective-permute-start | bytes 1769480 | tf_op jit(solution)/shard_map/ppermute | solution.py:12
  135.8 26.1 %collective-permute-start.7 = (f32[6,6,32,128]{3,2,0,1:T(8,128)S(1)}, f32[6,6,32,128]{3,2,0,1:T(8,128)S(1)}, u32[]{:S(2)}, u32[]{:S(2)}) collective-permute-start(f32[6,6,32,128]{3,2,0,1:T(8,128)S(1)} %dynamic-slice_add_fusion.8), channel_id=1, source_target_pairs={{0,6},{1,7},{2,0},{3,1},{4,2},{5,3},{6,4},{7,5},{8,14},{9,15},{10,... | collective-permute-start | bytes 1769480 | tf_op jit(solution)/shard_map/ppermute | solution.py:12
  139.2 26.6 %collective-permute-start.4 = (f32[6,6,32,128]{3,2,0,1:T(8,128)S(1)}, f32[6,6,32,128]{3,2,0,1:T(8,128)S(1)}, u32[]{:S(2)}, u32[]{:S(2)}) collective-permute-start(f32[6,6,32,128]{3,2,0,1:T(8,128)S(1)} %dynamic-slice_add_fusion.11), channel_id=1, source_target_pairs={{0,2},{1,3},{2,4},{3,5},{4,6},{5,7},{6,0},{7,1},{8,10},{9,11},{10,... | collective-permute-start | bytes 1769480 | tf_op jit(solution)/shard_map/ppermute | solution.py:12
  149.4 25.2 %collective-permute-start.14 = (f32[6,6,32,128]{3,2,0,1:T(8,128)S(1)}, f32[6,6,32,128]{3,2,0,1:T(8,128)S(1)}, u32[]{:S(2)}, u32[]{:S(2)}) collective-permute-start(f32[6,6,32,128]{3,2,0,1:T(8,128)S(1)} %dynamic-slice_add_fusion.2), channel_id=1, source_target_pairs={{0,6},{1,7},{2,0},{3,1},{4,2},{5,3},{6,4},{7,5},{8,14},{9,15},{10,... | collective-permute-start | bytes 1769480 | tf_op jit(solution)/shard_map/ppermute | solution.py:12
  153.2 25.2 %collective-permute-start.11 = (f32[6,6,32,128]{3,2,0,1:T(8,128)S(1)}, f32[6,6,32,128]{3,2,0,1:T(8,128)S(1)}, u32[]{:S(2)}, u32[]{:S(2)}) collective-permute-start(f32[6,6,32,128]{3,2,0,1:T(8,128)S(1)} %dynamic-slice_add_fusion.5), channel_id=1, source_target_pairs={{0,2},{1,3},{2,4},{3,5},{4,6},{5,7},{6,0},{7,1},{8,10},{9,11},{10,... | collective-permute-start | bytes 1769480 | tf_op jit(solution)/shard_map/ppermute | solution.py:12
  162.0 25.2 %collective-permute-start.8 = (f32[6,6,32,128]{3,2,0,1:T(8,128)S(1)}, f32[6,6,32,128]{3,2,0,1:T(8,128)S(1)}, u32[]{:S(2)}, u32[]{:S(2)}) collective-permute-start(f32[6,6,32,128]{3,2,0,1:T(8,128)S(1)} %dynamic-slice_add_fusion.7), channel_id=1, source_target_pairs={{0,6},{1,7},{2,0},{3,1},{4,2},{5,3},{6,4},{7,5},{8,14},{9,15},{10,... | collective-permute-start | bytes 1769480 | tf_op jit(solution)/shard_map/ppermute | solution.py:12
  165.9 25.1 %collective-permute-start.5 = (f32[6,6,32,128]{3,2,0,1:T(8,128)S(1)}, f32[6,6,32,128]{3,2,0,1:T(8,128)S(1)}, u32[]{:S(2)}, u32[]{:S(2)}) collective-permute-start(f32[6,6,32,128]{3,2,0,1:T(8,128)S(1)} %dynamic-slice_add_fusion.10), channel_id=1, source_target_pairs={{0,2},{1,3},{2,4},{3,5},{4,6},{5,7},{6,0},{7,1},{8,10},{9,11},{10,... | collective-permute-start | bytes 1769480 | tf_op jit(solution)/shard_map/ppermute | solution.py:12
  174.7 23.3 %collective-permute-start.15 = (f32[6,6,32,128]{3,2,0,1:T(8,128)S(1)}, f32[6,6,32,128]{3,2,0,1:T(8,128)S(1)}, u32[]{:S(2)}, u32[]{:S(2)}) collective-permute-start(f32[6,6,32,128]{3,2,0,1:T(8,128)S(1)} %dynamic-slice_add_fusion.1), channel_id=1, source_target_pairs={{0,6},{1,7},{2,0},{3,1},{4,2},{5,3},{6,4},{7,5},{8,14},{9,15},{10,... | collective-permute-start | bytes 1769480 | tf_op jit(solution)/shard_map/ppermute | solution.py:12
  178.5 23.0 %collective-permute-start.12 = (f32[6,6,32,128]{3,2,0,1:T(8,128)S(1)}, f32[6,6,32,128]{3,2,0,1:T(8,128)S(1)}, u32[]{:S(2)}, u32[]{:S(2)}) collective-permute-start(f32[6,6,32,128]{3,2,0,1:T(8,128)S(1)} %dynamic-slice_add_fusion.4), channel_id=1, source_target_pairs={{0,2},{1,3},{2,4},{3,5},{4,6},{5,7},{6,0},{7,1},{8,10},{9,11},{10,... | collective-permute-start | bytes 1769480 | tf_op jit(solution)/shard_map/ppermute | solution.py:12
  191.2 14.5 %collective-permute-start.9 = (f32[6,12,16,128]{3,2,0,1:T(8,128)S(1)}, f32[6,12,16,128]{3,2,0,1:T(8,128)S(1)}, u32[]{:S(2)}, u32[]{:S(2)}) collective-permute-start(f32[6,12,16,128]{3,2,0,1:T(8,128)S(1)} %fusion.13), channel_id=1, source_target_pairs={{0,1},{1,0},{2,3},{3,2},{4,5},{5,4},{6,7},{7,6},{8,9},{9,8},{10,11... | collective-permute-start | bytes 1769480 | tf_op jit(solution)/shard_map/ppermute | solution.py:12
  202.5 15.0 %collective-permute-start.16 = (f32[6,12,16,128]{3,2,0,1:T(8,128)}, f32[6,12,16,128]{3,2,0,1:T(8,128)}, u32[]{:S(2)}, u32[]{:S(2)}) collective-permute-start(f32[6,12,16,128]{3,2,0,1:T(8,128)} %fusion.10), channel_id=1, source_target_pairs={{0,1},{1,0},{2,3},{3,2},{4,5},{5,4},{6,7},{7,6},{8,9},{9,8},{10,11... | collective-permute-start | bytes 1769480 | tf_op jit(solution)/shard_map/ppermute | solution.py:12
  240.3 6.0 %collective-permute-start.17 = (f32[1,144,256]{2,1,0:T(8,128)S(1)}, f32[1,144,256]{2,1,0:T(8,128)S(1)}, u32[]{:S(2)}, u32[]{:S(2)}) collective-permute-start(f32[1,144,256]{2,1,0:T(8,128)S(1)} %get-tuple-element.16), channel_id=1, source_target_pairs={{0,0},{1,1},{2,2},{3,3},{4,4},{5,5},{6,6},{7,7},{8,32},{9,33},{10,... | collective-permute-start | bytes 442376 | tf_op jit(solution)/shard_map/ppermute | solution.py:101
  241.0 13.5 %collective-permute-start.18 = (f32[1,144,256]{2,1,0:T(8,128)S(1)}, f32[1,144,256]{2,1,0:T(8,128)S(1)}, u32[]{:S(2)}, u32[]{:S(2)}) collective-permute-start(f32[1,144,256]{2,1,0:T(8,128)S(1)} %get-tuple-element.15), channel_id=1, source_target_pairs={{0,1},{1,0},{2,3},{3,2},{4,5},{5,4},{6,7},{7,6},{8,33},{9,32},{10,... | collective-permute-start | bytes 442376 | tf_op jit(solution)/shard_map/ppermute | solution.py:101
  244.3 10.2 %collective-permute-start.19 = (f32[1,144,256]{2,1,0:T(8,128)S(1)}, f32[1,144,256]{2,1,0:T(8,128)S(1)}, u32[]{:S(2)}, u32[]{:S(2)}) collective-permute-start(f32[1,144,256]{2,1,0:T(8,128)S(1)} %get-tuple-element.14), channel_id=1, source_target_pairs={{0,2},{1,3},{2,0},{3,1},{4,6},{5,7},{6,4},{7,5},{8,34},{9,35},{10,... | collective-permute-start | bytes 442376 | tf_op jit(solution)/shard_map/ppermute | solution.py:101
  244.3 17.5 %collective-permute-start.20 = (f32[1,144,256]{2,1,0:T(8,128)S(1)}, f32[1,144,256]{2,1,0:T(8,128)S(1)}, u32[]{:S(2)}, u32[]{:S(2)}) collective-permute-start(f32[1,144,256]{2,1,0:T(8,128)S(1)} %get-tuple-element.13), channel_id=1, source_target_pairs={{0,3},{1,2},{2,1},{3,0},{4,7},{5,6},{6,5},{7,4},{8,35},{9,34},{10,... | collective-permute-start | bytes 442376 | tf_op jit(solution)/shard_map/ppermute | solution.py:101
  246.1 33.5 %collective-permute-start.21 = (f32[1,144,256]{2,1,0:T(8,128)S(1)}, f32[1,144,256]{2,1,0:T(8,128)S(1)}, u32[]{:S(2)}, u32[]{:S(2)}) collective-permute-start(f32[1,144,256]{2,1,0:T(8,128)S(1)} %get-tuple-element.12), channel_id=1, source_target_pairs={{0,4},{1,5},{2,6},{3,7},{4,0},{5,1},{6,2},{7,3},{8,36},{9,37},{10,... | collective-permute-start | bytes 442376 | tf_op jit(solution)/shard_map/ppermute | solution.py:101
  246.3 37.1 %collective-permute-start.22 = (f32[1,144,256]{2,1,0:T(8,128)S(1)}, f32[1,144,256]{2,1,0:T(8,128)S(1)}, u32[]{:S(2)}, u32[]{:S(2)}) collective-permute-start(f32[1,144,256]{2,1,0:T(8,128)S(1)} %get-tuple-element.11), channel_id=1, source_target_pairs={{0,5},{1,4},{2,7},{3,6},{4,1},{5,0},{6,3},{7,2},{8,37},{9,36},{10,... | collective-permute-start | bytes 442376 | tf_op jit(solution)/shard_map/ppermute | solution.py:101
  254.5 28.9 %collective-permute-start.23 = (f32[1,144,256]{2,1,0:T(8,128)S(1)}, f32[1,144,256]{2,1,0:T(8,128)S(1)}, u32[]{:S(2)}, u32[]{:S(2)}) collective-permute-start(f32[1,144,256]{2,1,0:T(8,128)S(1)} %get-tuple-element.10), channel_id=1, source_target_pairs={{0,6},{1,7},{2,4},{3,5},{4,2},{5,3},{6,0},{7,1},{8,38},{9,39},{10,... | collective-permute-start | bytes 442376 | tf_op jit(solution)/shard_map/ppermute | solution.py:101
  254.5 31.1 %collective-permute-start.24 = (f32[1,144,256]{2,1,0:T(8,128)S(1)}, f32[1,144,256]{2,1,0:T(8,128)S(1)}, u32[]{:S(2)}, u32[]{:S(2)}) collective-permute-start(f32[1,144,256]{2,1,0:T(8,128)S(1)} %get-tuple-element.9), channel_id=1, source_target_pairs={{0,7},{1,6},{2,5},{3,4},{4,3},{5,2},{6,1},{7,0},{8,39},{9,38},{10,... | collective-permute-start | bytes 442376 | tf_op jit(solution)/shard_map/ppermute | solution.py:101
Sparse Core Ops, SparseCore 0:
  11.8 94.2 all-gather.1
where the time goes:
time: 319 us; the launch traced here: 318 us
  waiting for transfers between devices  140 us (44%)
  local copies, waits for them, and re-layouts  69.5 us (22%)
  starting transfers between devices  48.4 us (15%)
  other arithmetic  22.4 us (7%)
  matrix products  21.7 us (7%)
  between operations  15.7 us (5%)
    ppermute x17, waiting for transfers between devices, shifted(): lax.ppermute(value, axis, [(src, fn(src) % size) for src in range(size)])  110 us
    ppermute x17, starting transfers between devices, shifted(): lax.ppermute(value, axis, [(src, fn(src) % size) for src in range(size)])  29.2 us
    ppermute x8, waiting for transfers between devices, body(): flat = lax.ppermute(flat, ('row', 'col', 'slab'), pairs)  25.8 us
    dot_general x2, matrix products, body(): jnp.einsum('ikca,kcjb->ijab', amp_part, int_abs, preferred_element_type=j...  21.7 us
    ppermute x8, starting transfers between devices, body(): flat = lax.ppermute(flat, ('row', 'col', 'slab'), pairs)  19.2 us
    reshape x2, local copies, waits for them, and re-layouts, body(): shares.reshape(i_n, j_n, a_n, n_slab, b_n // n_slab)  14.6 us
    transpose x1, local copies, waits for them, and re-layouts, body(): mirrored = jnp.transpose(gathered, (1, 2, 3, 0, 4)).reshape(shares.shape)  12.8 us
    select_n x1, other arithmetic, int_mask(): label_b = jnp.take(irreps, blocks + b_ids // VTILE)  11.8 us
  transfers between devices with their start and end apart: 26, of which 14 were waited for; matrix products, arithmetic and copies ran while one was open for 15% of the time, Pallas kernels for 0%

commit v1 on v0

--- a/solution.py
+++ b/solution.py
@@ -12,22 +12,24 @@
     return lax.ppermute(value, axis, [(src, fn(src) % size) for src in range(size)])
 
 
-def int_mask(irreps, blocks, row_at, col_at, slab_at, c_cols, win_cols):
+def int_mask(irreps, blocks, k_block, col_at, slab_at, c_cols, win_cols):
     c_ids = slab_at * c_cols + jnp.arange(c_cols, dtype=jnp.int32)
     b_ids = jnp.arange(win_cols, dtype=jnp.int32)
     label_c = jnp.take(irreps, blocks + c_ids // VTILE)
     label_b = jnp.take(irreps, blocks + b_ids // VTILE)
-    occ = irreps[row_at] + irreps[col_at]
+    occ = irreps[k_block] + irreps[col_at]
     parity = occ + label_c[:, None] + label_b[None, :]
     return parity % 2 == 0
 
 
-def gather_row(ints, row_at):
+def gather_row(ints, row_at, block_mask):
     zpart = shifted(ints, "row", lambda r: r ^ 2)
     blocks = [ints, shifted(ints, "row", lambda r: r ^ 1), zpart, shifted(zpart, "row", lambda r: r ^ 1)]
     k_rows = ints.shape[0]
     whole = jnp.zeros((len(blocks) * k_rows,) + ints.shape[1:], ints.dtype)
     for u, blk in enumerate(blocks):
+        mask = block_mask(row_at ^ u)
+        blk = jnp.where(mask[None, :, None, :], blk, jnp.zeros_like(blk))
         whole = lax.dynamic_update_slice_in_dim(whole, blk, (row_at ^ u) * k_rows, axis=0)
     return whole
 
@@ -64,11 +66,12 @@
 
     keep = pair_mask[row_at, col_at] != 0
     amp = jnp.where(keep, amplitudes, jnp.zeros_like(amplitudes))
-    mask = int_mask(irreps, blocks, row_at, col_at, slab_at, c_cols, win_cols)
-    ints = jnp.where(mask[None, :, None, :], integrals, jnp.zeros_like(integrals))
+    amp_all = lax.all_gather(amp, "col", axis=1, tiled=True)
 
-    amp_all = lax.all_gather(amp, "col", axis=1, tiled=True)
-    int_abs = gather_row(ints, row_at)
+    def block_mask(k_block):
+        return int_mask(irreps, blocks, k_block, col_at, slab_at, c_cols, win_cols)
+
+    int_abs = gather_row(integrals, row_at, block_mask)
     n_row = lax.axis_size("row")
     n_col = lax.axis_size("col")
     n_chunks = 2

time: 319 us -> 321 us (level)
  local copies, waits for them, and re-layouts: 69.5 us -> 59.2 us
  other arithmetic: 22.4 us -> 31 us
  between operations: 15.7 us -> 19.6 us
    dynamic_update_slice x1 -> x4, other arithmetic: 2.09 us -> 13.8 us  [gather_row(): lax.dynamic_update_slice_in_dim(whole, blk, (row_at ^ u) * k_rows, axis=0)]
    dynamic_update_slice x3 -> x0, local copies, waits for them, and re-layouts: 11.3 us -> none  [gather_row(): lax.dynamic_update_slice_in_dim(whole, blk, (row_at ^ u) * k_rows, axis=0)]
where the time goes in v1:
time: 321 us; the launch traced here: 320 us
  waiting for transfers between devices  137 us (43%)
  local copies, waits for them, and re-layouts  59.2 us (18%)
  starting transfers between devices  51.1 us (16%)
  other arithmetic  31 us (10%)
  matrix products  21.7 us (7%)
  between operations  19.6 us (6%)
    ppermute x17, waiting for transfers between devices, shifted(): lax.ppermute(value, axis, [(src, fn(src) % size) for src in range(size)])  109 us
    ppermute x17, starting transfers between devices, shifted(): lax.ppermute(value, axis, [(src, fn(src) % size) for src in range(size)])  32.2 us
    ppermute x8, waiting for transfers between devices, body(): flat = lax.ppermute(flat, ('row', 'col', 'slab'), pairs)  27.5 us
    dot_general x2, matrix products, body(): jnp.einsum('ikca,kcjb->ijab', amp_part, int_abs, preferred_element_type=j...  21.7 us
    ppermute x8, starting transfers between devices, body(): flat = lax.ppermute(flat, ('row', 'col', 'slab'), pairs)  18.9 us
    reshape x2, local copies, waits for them, and re-layouts, body(): shares.reshape(i_n, j_n, a_n, n_slab, b_n // n_slab)  14.6 us
    dynamic_update_slice x4, other arithmetic, gather_row(): lax.dynamic_update_slice_in_dim(whole, blk, (row_at ^ u) * k_rows, axis=0)  13.8 us
    transpose x1, local copies, waits for them, and re-layouts, body(): mirrored = jnp.transpose(gathered, (1, 2, 3, 0, 4)).reshape(shares.shape)  12.7 us
  transfers between devices with their start and end apart: 26, of which 14 were waited for; matrix products, arithmetic and copies ran while one was open for 15% of the time, Pallas kernels for 0%

profile of v1, /device:TPU:0, one launch (start us, length us, event | category | flops | bytes accessed | tf_op | source)
XLA Modules:
  0.0 319.9 jit_solution(17718663367474040112)
XLA Ops:
  15.0 50.2 %collective-permute-done.1 = bf16[12,60,12,128]{3,1,2,0:T(8,128)(2,1)} collective-permute-done((bf16[12,60,12,128]{3,1,2,0:T(8,128)(2,1)S(1)}, bf16[12,60,12,128]{3,1,2,0:T(8,128)(2,1)}, u32[]{:S(2)}, u32[]{:S(2)}) %collective-permute-start.1) | collective-permute-done | bytes 2211872 | tf_op jit(solution)/shard_map/ppermute | solution.py:12
  73.4 11.8 %and_select_fusion = s32[128]{0:T(128)S(1)} fusion(s32[]{:T(128)} %bitcast.19, s32[]{:T(128)} %bitcast.18, s32[]{:T(128)} %bitcast.17, s32[]{:T(128)} %bitcast.16, s32[]{:T(128)} %bitcast.15, s32[]{:T(128)} %bitcast.14, s32[]{:T(128)} %bitcast.13, s32[]{:T(128)} %bitcast.12, s32[]{:T(128)} %bitcast.11, s32[]{:T(128)} %bitcast.10, s32[]{:T(128)} %bitcast.9, ...), kind=kLoop, calls=%fused_computation.115 | loop fusion | flops 6656 | bytes 588 | tf_op jit(solution)/shard_map/jit(_take)/select_n | solution.py:19
  85.4 6.0 %broadcast_in_dim.56 = bf16[48,60,12,128]{3,1,0,2:T(8,128)(2,1)} broadcast(bf16[]{:T(256)} %constant.180.clone.1), dimensions={} | broadcast | bytes 8847362 | tf_op jit(solution)/shard_map/broadcast_in_dim | solution.py:29
  93.5 3.9 %copy_dynamic-update-slice_fusion.2 = bf16[48,60,12,128]{3,1,0,2:T(8,128)(2,1)} fusion(bf16[48,60,12,128]{3,1,0,2:T(8,128)(2,1)} %copy_dynamic-update-slice_fusion.3, s32[]{:T(128)S(6)} %select_n.249, bf16[12,60,12,128]{3,1,2,0:T(8,128)(2,1)} %collective-permute-done, pred[60,128]{1,0:T(8,128)(4,1)S(1)} %get-tuple-element.22), kind=kLoop, calls=%fused_computation.9 | loop fusion | flops 1105920 | bytes 4726276 | tf_op jit(solution)/shard_map/dynamic_update_slice | solution.py:33
  97.4 3.9 %copy_dynamic-update-slice_fusion.1 = bf16[48,60,12,128]{3,1,0,2:T(8,128)(2,1)} fusion(bf16[48,60,12,128]{3,1,0,2:T(8,128)(2,1)} %copy_dynamic-update-slice_fusion.2, s32[]{:T(128)S(6)} %select_n.253, bf16[12,60,12,128]{3,1,2,0:T(8,128)(2,1)} %collective-permute-done.1, pred[60,128]{1,0:T(8,128)(4,1)S(1)} %get-tuple-element.23), kind=kLoop, calls=%fused_computation.8 | loop fusion | flops 1105920 | bytes 4726276 | tf_op jit(solution)/shard_map/dynamic_update_slice | solution.py:33
  101.3 3.9 %copy_dynamic-update-slice_fusion = bf16[48,60,12,128]{3,1,0,2:T(8,128)(2,1)} fusion(bf16[48,60,12,128]{3,1,0,2:T(8,128)(2,1)} %copy_dynamic-update-slice_fusion.1, s32[]{:T(128)S(6)} %select_n.257, bf16[12,60,12,128]{3,1,2,0:T(8,128)(2,1)} %collective-permute-done.2, pred[60,128]{1,0:T(8,128)(4,1)S(1)} %get-tuple-element.21), kind=kLoop, calls=%fused_computation.7 | loop fusion | flops 1105920 | bytes 4726276 | tf_op jit(solution)/shard_map/dynamic_update_slice | solution.py:33
  106.3 11.6 %fusion.4 = f32[6,12,128,128]{3,2,0,1:T(8,128)S(1)} fusion(bf16[12,48,60,128]{3,2,1,0:T(8,128)(2,1)} %all-gather.2.cloned.1.call-done, bf16[48,60,12,128]{3,1,0,2:T(8,128)(2,1)} %copy_dynamic-update-slice_fusion), kind=kOutput, calls=%fused_computation.16 | convolution fusion | flops 6794772480 | bytes 18874368 | tf_op jit(solution)/shard_map/ikca,kcjb->ijab/dot_general | solution.py:82
  121.7 10.1 %fusion.7 = f32[6,12,128,128]{3,2,0,1:T(8,128)S(1)} fusion(bf16[12,48,60,128]{3,2,1,0:T(8,128)(2,1)S(1)} %copy-done.2, bf16[48,60,12,128]{3,1,0,2:T(8,128)(2,1)} %copy_dynamic-update-slice_fusion), kind=kOutput, calls=%fused_computation.17 | convolution fusion | flops 6794772480 | bytes 18284544 | tf_op jit(solution)/shard_map/ikca,kcjb->ijab/dot_general | solution.py:82
  139.5 10.0 %collective-permute-done.13 = f32[6,6,32,128]{3,2,0,1:T(8,128)S(1)} collective-permute-done((f32[6,6,32,128]{3,2,0,1:T(8,128)S(1)}, f32[6,6,32,128]{3,2,0,1:T(8,128)S(1)}, u32[]{:S(2)}, u32[]{:S(2)}) %collective-permute-start.13) | collective-permute-done | bytes 589856 | tf_op jit(solution)/shard_map/ppermute | solution.py:12
  149.6 3.8 %collective-permute-start.14 = (f32[6,6,32,128]{3,2,0,1:T(8,128)S(1)}, f32[6,6,32,128]{3,2,0,1:T(8,128)S(1)}, u32[]{:S(2)}, u32[]{:S(2)}) collective-permute-start(f32[6,6,32,128]{3,2,0,1:T(8,128)S(1)} %dynamic-slice_add_fusion.2), channel_id=1, source_target_pairs={{0,6},{1,7},{2,0},{3,1},{4,2},{5,3},{6,4},{7,5},{8,14},{9,15},{10,... | collective-permute-start | bytes 1769480 | tf_op jit(solution)/shard_map/ppermute | solution.py:12
  153.5 8.6 %collective-permute-done.7 = f32[6,6,32,128]{3,2,0,1:T(8,128)S(1)} collective-permute-done((f32[6,6,32,128]{3,2,0,1:T(8,128)S(1)}, f32[6,6,32,128]{3,2,0,1:T(8,128)S(1)}, u32[]{:S(2)}, u32[]{:S(2)}) %collective-permute-start.7) | collective-permute-done | bytes 589856 | tf_op jit(solution)/shard_map/ppermute | solution.py:12
  162.2 3.8 %collective-permute-start.8 = (f32[6,6,32,128]{3,2,0,1:T(8,128)S(1)}, f32[6,6,32,128]{3,2,0,1:T(8,128)S(1)}, u32[]{:S(2)}, u32[]{:S(2)}) collective-permute-start(f32[6,6,32,128]{3,2,0,1:T(8,128)S(1)} %dynamic-slice_add_fusion.7), channel_id=1, source_target_pairs={{0,6},{1,7},{2,0},{3,1},{4,2},{5,3},{6,4},{7,5},{8,14},{9,15},{10,... | collective-permute-start | bytes 1769480 | tf_op jit(solution)/shard_map/ppermute | solution.py:12
  166.2 8.6 %collective-permute-done.14 = f32[6,6,32,128]{3,2,0,1:T(8,128)S(1)} collective-permute-done((f32[6,6,32,128]{3,2,0,1:T(8,128)S(1)}, f32[6,6,32,128]{3,2,0,1:T(8,128)S(1)}, u32[]{:S(2)}, u32[]{:S(2)}) %collective-permute-start.14) | collective-permute-done | bytes 589856 | tf_op jit(solution)/shard_map/ppermute | solution.py:12
  174.8 3.8 %collective-permute-start.15 = (f32[6,6,32,128]{3,2,0,1:T(8,128)S(1)}, f32[6,6,32,128]{3,2,0,1:T(8,128)S(1)}, u32[]{:S(2)}, u32[]{:S(2)}) collective-permute-start(f32[6,6,32,128]{3,2,0,1:T(8,128)S(1)} %dynamic-slice_add_fusion.1), channel_id=1, source_target_pairs={{0,6},{1,7},{2,0},{3,1},{4,2},{5,3},{6,4},{7,5},{8,14},{9,15},{10,... | collective-permute-start | bytes 1769480 | tf_op jit(solution)/shard_map/ppermute | solution.py:12
  178.8 8.6 %collective-permute-done.8 = f32[6,6,32,128]{3,2,0,1:T(8,128)S(1)} collective-permute-done((f32[6,6,32,128]{3,2,0,1:T(8,128)S(1)}, f32[6,6,32,128]{3,2,0,1:T(8,128)S(1)}, u32[]{:S(2)}, u32[]{:S(2)}) %collective-permute-start.8) | collective-permute-done | bytes 589856 | tf_op jit(solution)/shard_map/ppermute | solution.py:12
  187.5 3.7 %collective-permute-done.5 = f32[6,6,32,128]{3,2,0,1:T(8,128)S(1)} collective-permute-done((f32[6,6,32,128]{3,2,0,1:T(8,128)S(1)}, f32[6,6,32,128]{3,2,0,1:T(8,128)S(1)}, u32[]{:S(2)}, u32[]{:S(2)}) %collective-permute-start.5) | collective-permute-done | bytes 589856 | tf_op jit(solution)/shard_map/ppermute | solution.py:12
  194.6 3.6 %collective-permute-done.15 = f32[6,6,32,128]{3,2,0,1:T(8,128)S(1)} collective-permute-done((f32[6,6,32,128]{3,2,0,1:T(8,128)S(1)}, f32[6,6,32,128]{3,2,0,1:T(8,128)S(1)}, u32[]{:S(2)}, u32[]{:S(2)}) %collective-permute-start.15) | collective-permute-done | bytes 589856 | tf_op jit(solution)/shard_map/ppermute | solution.py:12
  198.3 3.4 %collective-permute-done.12 = f32[6,6,32,128]{3,2,0,1:T(8,128)S(1)} collective-permute-done((f32[6,6,32,128]{3,2,0,1:T(8,128)S(1)}, f32[6,6,32,128]{3,2,0,1:T(8,128)S(1)}, u32[]{:S(2)}, u32[]{:S(2)}) %collective-permute-start.12) | collective-permute-done | bytes 589856 | tf_op jit(solution)/shard_map/ppermute | solution.py:12
  202.7 3.5 %collective-permute-start.16 = (f32[6,12,16,128]{3,2,0,1:T(8,128)}, f32[6,12,16,128]{3,2,0,1:T(8,128)}, u32[]{:S(2)}, u32[]{:S(2)}) collective-permute-start(f32[6,12,16,128]{3,2,0,1:T(8,128)} %fusion.10), channel_id=1, source_target_pairs={{0,1},{1,0},{2,3},{3,2},{4,5},{5,4},{6,7},{7,6},{8,9},{9,8},{10,11... | collective-permute-start | bytes 1769480 | tf_op jit(solution)/shard_map/ppermute | solution.py:12
  206.3 12.0 %collective-permute-done.16 = f32[6,12,16,128]{3,2,0,1:T(8,128)} collective-permute-done((f32[6,12,16,128]{3,2,0,1:T(8,128)}, f32[6,12,16,128]{3,2,0,1:T(8,128)}, u32[]{:S(2)}, u32[]{:S(2)}) %collective-permute-start.16) | collective-permute-done | bytes 589856 | tf_op jit(solution)/shard_map/ppermute | solution.py:12
  219.5 5.0 %reshape.178 = f32[12,12,16,8,16]{4,3,2,0,1:T(8,128)} reshape(f32[12,12,16,128]{3,2,0,1:T(8,128)S(1)} %pad_maximum_fusion) | data formatting | bytes 2359296 | tf_op jit(solution)/shard_map/reshape | solution.py:93
  224.5 9.6 %copy.14 = f32[12,12,16,8,16]{2,4,0,1,3:T(8,128)} copy(f32[12,12,16,8,16]{4,3,2,0,1:T(8,128)} %reshape.178) | data formatting | bytes 2359296 | tf_op jit(solution)/shard_map/reshape | solution.py:93
  234.1 6.9 %reshape.179 = f32[8,144,256]{2,1,0:T(8,128)S(1)} reshape(f32[8,12,12,16,16]{4,3,2,1,0:T(8,128)} %bitcast.67) | data formatting | bytes 2359296 | tf_op jit(solution)/shard_map/reshape | solution.py:94
  247.2 5.9 %collective-permute-start.22 = (f32[1,144,256]{2,1,0:T(8,128)S(1)}, f32[1,144,256]{2,1,0:T(8,128)S(1)}, u32[]{:S(2)}, u32[]{:S(2)}) collective-permute-start(f32[1,144,256]{2,1,0:T(8,128)S(1)} %get-tuple-element.15), channel_id=1, source_target_pairs={{0,5},{1,4},{2,7},{3,6},{4,1},{5,0},{6,3},{7,2},{8,37},{9,36},{10,... | collective-permute-start | bytes 442376 | tf_op jit(solution)/shard_map/ppermute | solution.py:104
  253.2 5.2 %collective-permute-done.18 = f32[1,144,256]{2,1,0:T(8,128)S(1)} collective-permute-done((f32[1,144,256]{2,1,0:T(8,128)S(1)}, f32[1,144,256]{2,1,0:T(8,128)S(1)}, u32[]{:S(2)}, u32[]{:S(2)}) %collective-permute-start.18) | collective-permute-done | bytes 147488 | tf_op jit(solution)/shard_map/ppermute | solution.py:104
  258.5 7.0 %collective-permute-start.24 = (f32[1,144,256]{2,1,0:T(8,128)S(1)}, f32[1,144,256]{2,1,0:T(8,128)S(1)}, u32[]{:S(2)}, u32[]{:S(2)}) collective-permute-start(f32[1,144,256]{2,1,0:T(8,128)S(1)} %get-tuple-element.13), channel_id=1, source_target_pairs={{0,7},{1,6},{2,5},{3,4},{4,3},{5,2},{6,1},{7,0},{8,39},{9,38},{10,... | collective-permute-start | bytes 442376 | tf_op jit(solution)/shard_map/ppermute | solution.py:104
  265.5 12.7 %collective-permute-done.21 = f32[1,144,256]{2,1,0:T(8,128)S(1)} collective-permute-done((f32[1,144,256]{2,1,0:T(8,128)S(1)}, f32[1,144,256]{2,1,0:T(8,128)S(1)}, u32[]{:S(2)}, u32[]{:S(2)}) %collective-permute-start.21) | collective-permute-done | bytes 147488 | tf_op jit(solution)/shard_map/ppermute | solution.py:104
  278.2 5.5 %collective-permute-done.22 = f32[1,144,256]{2,1,0:T(8,128)S(1)} collective-permute-done((f32[1,144,256]{2,1,0:T(8,128)S(1)}, f32[1,144,256]{2,1,0:T(8,128)S(1)}, u32[]{:S(2)}, u32[]{:S(2)}) %collective-permute-start.22) | collective-permute-done | bytes 147488 | tf_op jit(solution)/shard_map/ppermute | solution.py:104
  283.8 4.0 %collective-permute-done.24 = f32[1,144,256]{2,1,0:T(8,128)S(1)} collective-permute-done((f32[1,144,256]{2,1,0:T(8,128)S(1)}, f32[1,144,256]{2,1,0:T(8,128)S(1)}, u32[]{:S(2)}, u32[]{:S(2)}) %collective-permute-start.24) | collective-permute-done | bytes 147488 | tf_op jit(solution)/shard_map/ppermute | solution.py:104
  287.8 5.1 %reshape.180 = f32[8,12,12,16,16]{4,3,2,1,0:T(8,128)} reshape(f32[8,144,256]{2,1,0:T(8,128)S(1)} %constant_dynamic-update-slice_fusion) | data formatting | bytes 2359296 | tf_op jit(solution)/shard_map/reshape | solution.py:106
  293.0 12.7 %copy.15 = f32[12,12,16,8,16]{4,3,2,0,1:T(8,128)} copy(f32[12,12,16,8,16]{4,2,1,0,3:T(8,128)} %bitcast.68) | data formatting | bytes 2359296 | tf_op jit(solution)/shard_map/transpose | solution.py:107
  305.7 6.2 %reshape.181 = f32[12,12,16,128]{3,2,0,1:T(8,128)S(1)} reshape(f32[12,12,16,8,16]{4,3,2,0,1:T(8,128)} %copy.15) | data formatting | bytes 2359296 | tf_op jit(solution)/shard_map/reshape | solution.py:107
  (86 shorter events, 39.7 us)
Async XLA Ops:
  6.5 99.8 %all-gather.2.cloned.1.call-start = ((), (), s32[]{:S(2)}) async-start(), calls=%async_computation | async-start | bytes 11796480 | tf_op jit(solution)/shard_map/all_gather | solution.py:69
  10.1 1.7 copy-start.1
  10.1 56.2 %copy-start = (s32[19]{0:T(128)S(1)}, s32[19]{0:T(128)}, u32[]{:S(2)}) copy-start(s32[19]{0:T(128)} %param.10) | copy-start | bytes 232
  11.7 53.4 %collective-permute-start.1 = (bf16[12,60,12,128]{3,1,2,0:T(8,128)(2,1)S(1)}, bf16[12,60,12,128]{3,1,2,0:T(8,128)(2,1)}, u32[]{:S(2)}, u32[]{:S(2)}) collective-permute-start(bf16[12,60,12,128]{3,1,2,0:T(8,128)(2,1)S(1)} %copy-done.1), channel_id=1, source_target_pairs={{0,64},{32,96},{64,0},{96,32},{1,65},{33,97},{65,1},{97,33},{2,66}... | collective-permute-start | bytes 6635528 | tf_op jit(solution)/shard_map/ppermute | solution.py:12
  13.8 79.7 %collective-permute-start = (bf16[12,60,12,128]{3,1,2,0:T(8,128)(2,1)S(1)}, bf16[12,60,12,128]{3,1,2,0:T(8,128)(2,1)}, u32[]{:S(2)}, u32[]{:S(2)}) collective-permute-start(bf16[12,60,12,128]{3,1,2,0:T(8,128)(2,1)S(1)} %copy-done.1), channel_id=1, source_target_pairs={{0,32},{32,0},{64,96},{96,64},{1,33},{33,1},{65,97},{97,65},{2,34}... | collective-permute-start | bytes 6635528 | tf_op jit(solution)/shard_map/ppermute | solution.py:12
  65.2 36.2 %collective-permute-start.2 = (bf16[12,60,12,128]{3,1,2,0:T(8,128)(2,1)}, bf16[12,60,12,128]{3,1,2,0:T(8,128)(2,1)}, u32[]{:S(2)}, u32[]{:S(2)}) collective-permute-start(bf16[12,60,12,128]{3,1,2,0:T(8,128)(2,1)} %collective-permute-done.1), channel_id=1, source_target_pairs={{0,32},{32,0},{64,96},{96,64},{1,33},{33,1},{65,97},{97,65},{2,34}... | collective-permute-start | bytes 6635528 | tf_op jit(solution)/shard_map/ppermute | solution.py:12
  117.9 3.8 %copy-start.2 = (bf16[12,48,60,128]{3,2,1,0:T(8,128)(2,1)S(1)}, bf16[12,48,60,128]{3,2,1,0:T(8,128)(2,1)}, u32[]{:S(2)}) copy-start(bf16[12,48,60,128]{3,2,1,0:T(8,128)(2,1)} %all-gather.2.cloned.1.call-done) | copy-start | bytes 26542084
  118.5 17.3 %collective-permute-start.6 = (f32[6,6,32,128]{3,2,0,1:T(8,128)S(1)}, f32[6,6,32,128]{3,2,0,1:T(8,128)S(1)}, u32[]{:S(2)}, u32[]{:S(2)}) collective-permute-start(f32[6,6,32,128]{3,2,0,1:T(8,128)S(1)} %constant_dynamic-slice_fusion.10), channel_id=1, source_target_pairs={{0,6},{1,7},{2,0},{3,1},{4,2},{5,3},{6,4},{7,5},{8,14},{9,15},{10,... | collective-permute-start | bytes 1769480 | tf_op jit(solution)/shard_map/ppermute | solution.py:12
  121.4 17.9 %collective-permute-start.3 = (f32[6,6,32,128]{3,2,0,1:T(8,128)S(1)}, f32[6,6,32,128]{3,2,0,1:T(8,128)S(1)}, u32[]{:S(2)}, u32[]{:S(2)}) collective-permute-start(f32[6,6,32,128]{3,2,0,1:T(8,128)S(1)} %constant_dynamic-slice_fusion.11), channel_id=1, source_target_pairs={{0,2},{1,3},{2,4},{3,5},{4,6},{5,7},{6,0},{7,1},{8,10},{9,11},{10,... | collective-permute-start | bytes 1769480 | tf_op jit(solution)/shard_map/ppermute | solution.py:12
  132.5 17.0 %collective-permute-start.13 = (f32[6,6,32,128]{3,2,0,1:T(8,128)S(1)}, f32[6,6,32,128]{3,2,0,1:T(8,128)S(1)}, u32[]{:S(2)}, u32[]{:S(2)}) collective-permute-start(f32[6,6,32,128]{3,2,0,1:T(8,128)S(1)} %constant_dynamic-slice_fusion.8), channel_id=1, source_target_pairs={{0,6},{1,7},{2,0},{3,1},{4,2},{5,3},{6,4},{7,5},{8,14},{9,15},{10,... | collective-permute-start | bytes 1769480 | tf_op jit(solution)/shard_map/ppermute | solution.py:12
  135.8 17.5 %collective-permute-start.10 = (f32[6,6,32,128]{3,2,0,1:T(8,128)S(1)}, f32[6,6,32,128]{3,2,0,1:T(8,128)S(1)}, u32[]{:S(2)}, u32[]{:S(2)}) collective-permute-start(f32[6,6,32,128]{3,2,0,1:T(8,128)S(1)} %constant_dynamic-slice_fusion.9), channel_id=1, source_target_pairs={{0,2},{1,3},{2,4},{3,5},{4,6},{5,7},{6,0},{7,1},{8,10},{9,11},{10,... | collective-permute-start | bytes 1769480 | tf_op jit(solution)/shard_map/ppermute | solution.py:12
  136.0 26.1 %collective-permute-start.7 = (f32[6,6,32,128]{3,2,0,1:T(8,128)S(1)}, f32[6,6,32,128]{3,2,0,1:T(8,128)S(1)}, u32[]{:S(2)}, u32[]{:S(2)}) collective-permute-start(f32[6,6,32,128]{3,2,0,1:T(8,128)S(1)} %dynamic-slice_add_fusion.8), channel_id=1, source_target_pairs={{0,6},{1,7},{2,0},{3,1},{4,2},{5,3},{6,4},{7,5},{8,14},{9,15},{10,... | collective-permute-start | bytes 1769480 | tf_op jit(solution)/shard_map/ppermute | solution.py:12
  139.4 26.6 %collective-permute-start.4 = (f32[6,6,32,128]{3,2,0,1:T(8,128)S(1)}, f32[6,6,32,128]{3,2,0,1:T(8,128)S(1)}, u32[]{:S(2)}, u32[]{:S(2)}) collective-permute-start(f32[6,6,32,128]{3,2,0,1:T(8,128)S(1)} %dynamic-slice_add_fusion.11), channel_id=1, source_target_pairs={{0,2},{1,3},{2,4},{3,5},{4,6},{5,7},{6,0},{7,1},{8,10},{9,11},{10,... | collective-permute-start | bytes 1769480 | tf_op jit(solution)/shard_map/ppermute | solution.py:12
  149.6 25.2 %collective-permute-start.14 = (f32[6,6,32,128]{3,2,0,1:T(8,128)S(1)}, f32[6,6,32,128]{3,2,0,1:T(8,128)S(1)}, u32[]{:S(2)}, u32[]{:S(2)}) collective-permute-start(f32[6,6,32,128]{3,2,0,1:T(8,128)S(1)} %dynamic-slice_add_fusion.2), channel_id=1, source_target_pairs={{0,6},{1,7},{2,0},{3,1},{4,2},{5,3},{6,4},{7,5},{8,14},{9,15},{10,... | collective-permute-start | bytes 1769480 | tf_op jit(solution)/shard_map/ppermute | solution.py:12
  153.4 25.2 %collective-permute-start.11 = (f32[6,6,32,128]{3,2,0,1:T(8,128)S(1)}, f32[6,6,32,128]{3,2,0,1:T(8,128)S(1)}, u32[]{:S(2)}, u32[]{:S(2)}) collective-permute-start(f32[6,6,32,128]{3,2,0,1:T(8,128)S(1)} %dynamic-slice_add_fusion.5), channel_id=1, source_target_pairs={{0,2},{1,3},{2,4},{3,5},{4,6},{5,7},{6,0},{7,1},{8,10},{9,11},{10,... | collective-permute-start | bytes 1769480 | tf_op jit(solution)/shard_map/ppermute | solution.py:12
  162.2 25.2 %collective-permute-start.8 = (f32[6,6,32,128]{3,2,0,1:T(8,128)S(1)}, f32[6,6,32,128]{3,2,0,1:T(8,128)S(1)}, u32[]{:S(2)}, u32[]{:S(2)}) collective-permute-start(f32[6,6,32,128]{3,2,0,1:T(8,128)S(1)} %dynamic-slice_add_fusion.7), channel_id=1, source_target_pairs={{0,6},{1,7},{2,0},{3,1},{4,2},{5,3},{6,4},{7,5},{8,14},{9,15},{10,... | collective-permute-start | bytes 1769480 | tf_op jit(solution)/shard_map/ppermute | solution.py:12
  166.1 25.1 %collective-permute-start.5 = (f32[6,6,32,128]{3,2,0,1:T(8,128)S(1)}, f32[6,6,32,128]{3,2,0,1:T(8,128)S(1)}, u32[]{:S(2)}, u32[]{:S(2)}) collective-permute-start(f32[6,6,32,128]{3,2,0,1:T(8,128)S(1)} %dynamic-slice_add_fusion.10), channel_id=1, source_target_pairs={{0,2},{1,3},{2,4},{3,5},{4,6},{5,7},{6,0},{7,1},{8,10},{9,11},{10,... | collective-permute-start | bytes 1769480 | tf_op jit(solution)/shard_map/ppermute | solution.py:12
  174.8 23.3 %collective-permute-start.15 = (f32[6,6,32,128]{3,2,0,1:T(8,128)S(1)}, f32[6,6,32,128]{3,2,0,1:T(8,128)S(1)}, u32[]{:S(2)}, u32[]{:S(2)}) collective-permute-start(f32[6,6,32,128]{3,2,0,1:T(8,128)S(1)} %dynamic-slice_add_fusion.1), channel_id=1, source_target_pairs={{0,6},{1,7},{2,0},{3,1},{4,2},{5,3},{6,4},{7,5},{8,14},{9,15},{10,... | collective-permute-start | bytes 1769480 | tf_op jit(solution)/shard_map/ppermute | solution.py:12
  178.7 23.0 %collective-permute-start.12 = (f32[6,6,32,128]{3,2,0,1:T(8,128)S(1)}, f32[6,6,32,128]{3,2,0,1:T(8,128)S(1)}, u32[]{:S(2)}, u32[]{:S(2)}) collective-permute-start(f32[6,6,32,128]{3,2,0,1:T(8,128)S(1)} %dynamic-slice_add_fusion.4), channel_id=1, source_target_pairs={{0,2},{1,3},{2,4},{3,5},{4,6},{5,7},{6,0},{7,1},{8,10},{9,11},{10,... | collective-permute-start | bytes 1769480 | tf_op jit(solution)/shard_map/ppermute | solution.py:12
  191.4 14.8 %collective-permute-start.9 = (f32[6,12,16,128]{3,2,0,1:T(8,128)S(1)}, f32[6,12,16,128]{3,2,0,1:T(8,128)S(1)}, u32[]{:S(2)}, u32[]{:S(2)}) collective-permute-start(f32[6,12,16,128]{3,2,0,1:T(8,128)S(1)} %fusion.13), channel_id=1, source_target_pairs={{0,1},{1,0},{2,3},{3,2},{4,5},{5,4},{6,7},{7,6},{8,9},{9,8},{10,11... | collective-permute-start | bytes 1769480 | tf_op jit(solution)/shard_map/ppermute | solution.py:12
  202.7 15.6 %collective-permute-start.16 = (f32[6,12,16,128]{3,2,0,1:T(8,128)}, f32[6,12,16,128]{3,2,0,1:T(8,128)}, u32[]{:S(2)}, u32[]{:S(2)}) collective-permute-start(f32[6,12,16,128]{3,2,0,1:T(8,128)} %fusion.10), channel_id=1, source_target_pairs={{0,1},{1,0},{2,3},{3,2},{4,5},{5,4},{6,7},{7,6},{8,9},{9,8},{10,11... | collective-permute-start | bytes 1769480 | tf_op jit(solution)/shard_map/ppermute | solution.py:12
  241.1 6.1 %collective-permute-start.17 = (f32[1,144,256]{2,1,0:T(8,128)S(1)}, f32[1,144,256]{2,1,0:T(8,128)S(1)}, u32[]{:S(2)}, u32[]{:S(2)}) collective-permute-start(f32[1,144,256]{2,1,0:T(8,128)S(1)} %get-tuple-element.20), channel_id=1, source_target_pairs={{0,0},{1,1},{2,2},{3,3},{4,4},{5,5},{6,6},{7,7},{8,32},{9,33},{10,... | collective-permute-start | bytes 442376 | tf_op jit(solution)/shard_map/ppermute | solution.py:104
  241.8 16.7 %collective-permute-start.18 = (f32[1,144,256]{2,1,0:T(8,128)S(1)}, f32[1,144,256]{2,1,0:T(8,128)S(1)}, u32[]{:S(2)}, u32[]{:S(2)}) collective-permute-start(f32[1,144,256]{2,1,0:T(8,128)S(1)} %get-tuple-element.19), channel_id=1, source_target_pairs={{0,1},{1,0},{2,3},{3,2},{4,5},{5,4},{6,7},{7,6},{8,33},{9,32},{10,... | collective-permute-start | bytes 442376 | tf_op jit(solution)/shard_map/ppermute | solution.py:104
  245.1 13.4 %collective-permute-start.19 = (f32[1,144,256]{2,1,0:T(8,128)S(1)}, f32[1,144,256]{2,1,0:T(8,128)S(1)}, u32[]{:S(2)}, u32[]{:S(2)}) collective-permute-start(f32[1,144,256]{2,1,0:T(8,128)S(1)} %get-tuple-element.18), channel_id=1, source_target_pairs={{0,2},{1,3},{2,0},{3,1},{4,6},{5,7},{6,4},{7,5},{8,34},{9,35},{10,... | collective-permute-start | bytes 442376 | tf_op jit(solution)/shard_map/ppermute | solution.py:104
  245.1 20.3 %collective-permute-start.20 = (f32[1,144,256]{2,1,0:T(8,128)S(1)}, f32[1,144,256]{2,1,0:T(8,128)S(1)}, u32[]{:S(2)}, u32[]{:S(2)}) collective-permute-start(f32[1,144,256]{2,1,0:T(8,128)S(1)} %get-tuple-element.17), channel_id=1, source_target_pairs={{0,3},{1,2},{2,1},{3,0},{4,7},{5,6},{6,5},{7,4},{8,35},{9,34},{10,... | collective-permute-start | bytes 442376 | tf_op jit(solution)/shard_map/ppermute | solution.py:104
  246.8 31.4 %collective-permute-start.21 = (f32[1,144,256]{2,1,0:T(8,128)S(1)}, f32[1,144,256]{2,1,0:T(8,128)S(1)}, u32[]{:S(2)}, u32[]{:S(2)}) collective-permute-start(f32[1,144,256]{2,1,0:T(8,128)S(1)} %get-tuple-element.16), channel_id=1, source_target_pairs={{0,4},{1,5},{2,6},{3,7},{4,0},{5,1},{6,2},{7,3},{8,36},{9,37},{10,... | collective-permute-start | bytes 442376 | tf_op jit(solution)/shard_map/ppermute | solution.py:104
  247.2 36.6 %collective-permute-start.22 = (f32[1,144,256]{2,1,0:T(8,128)S(1)}, f32[1,144,256]{2,1,0:T(8,128)S(1)}, u32[]{:S(2)}, u32[]{:S(2)}) collective-permute-start(f32[1,144,256]{2,1,0:T(8,128)S(1)} %get-tuple-element.15), channel_id=1, source_target_pairs={{0,5},{1,4},{2,7},{3,6},{4,1},{5,0},{6,3},{7,2},{8,37},{9,36},{10,... | collective-permute-start | bytes 442376 | tf_op jit(solution)/shard_map/ppermute | solution.py:104
  258.5 25.3 %collective-permute-start.23 = (f32[1,144,256]{2,1,0:T(8,128)S(1)}, f32[1,144,256]{2,1,0:T(8,128)S(1)}, u32[]{:S(2)}, u32[]{:S(2)}) collective-permute-start(f32[1,144,256]{2,1,0:T(8,128)S(1)} %get-tuple-element.14), channel_id=1, source_target_pairs={{0,6},{1,7},{2,4},{3,5},{4,2},{5,3},{6,0},{7,1},{8,38},{9,39},{10,... | collective-permute-start | bytes 442376 | tf_op jit(solution)/shard_map/ppermute | solution.py:104
  258.5 29.3 %collective-permute-start.24 = (f32[1,144,256]{2,1,0:T(8,128)S(1)}, f32[1,144,256]{2,1,0:T(8,128)S(1)}, u32[]{:S(2)}, u32[]{:S(2)}) collective-permute-start(f32[1,144,256]{2,1,0:T(8,128)S(1)} %get-tuple-element.13), channel_id=1, source_target_pairs={{0,7},{1,6},{2,5},{3,4},{4,3},{5,2},{6,1},{7,0},{8,39},{9,38},{10,... | collective-permute-start | bytes 442376 | tf_op jit(solution)/shard_map/ppermute | solution.py:104
Sparse Core Ops, SparseCore 0:
  10.2 96.0 all-gather.1

commit v2 on v0

--- a/solution.py
+++ b/solution.py
@@ -29,6 +29,20 @@
     whole = jnp.zeros((len(blocks) * k_rows,) + ints.shape[1:], ints.dtype)
     for u, blk in enumerate(blocks):
         whole = lax.dynamic_update_slice_in_dim(whole, blk, (row_at ^ u) * k_rows, axis=0)
+    return whole
+
+
+def gather_col_rows(amp, col_at):
+    near1 = shifted(amp, "col", lambda c: c ^ 1)
+    near3 = shifted(amp, "col", lambda c: c ^ 3)
+    half = amp.shape[0] // 2
+    far_a = shifted(near3[:half], "col", lambda c: c ^ 1)
+    far_b = shifted(near1[half:], "col", lambda c: c ^ 3)
+    far = jnp.concatenate([far_a, far_b], axis=0)
+    k_rows = amp.shape[1]
+    whole = jnp.zeros((amp.shape[0], 4 * k_rows) + amp.shape[2:], amp.dtype)
+    for v, blk in enumerate([amp, near1, far, near3]):
+        whole = lax.dynamic_update_slice_in_dim(whole, blk, (col_at ^ v) * k_rows, axis=1)
     return whole
 
 
@@ -67,7 +81,14 @@
     mask = int_mask(irreps, blocks, row_at, col_at, slab_at, c_cols, win_cols)
     ints = jnp.where(mask[None, :, None, :], integrals, jnp.zeros_like(integrals))
 
-    amp_all = lax.all_gather(amp, "col", axis=1, tiled=True)
+    sc_rows = 2 * i_rows // 3
+    amp_all = jnp.concatenate(
+        [
+            lax.all_gather(amp[:sc_rows], "col", axis=1, tiled=True),
+            gather_col_rows(amp[sc_rows:], col_at),
+        ],
+        axis=0,
+    )
     int_abs = gather_row(ints, row_at)
     n_row = lax.axis_size("row")
     n_col = lax.axis_size("col")

time: 319 us -> 337 us (1.056); the launches traced: 318 us -> 331 us
  local copies, waits for them, and re-layouts: 69.5 us -> 81.8 us
  waiting for transfers between devices: 140 us -> 135 us
  starting transfers between devices: 48.4 us -> 52.5 us
    ppermute x17 -> x21, starting transfers between devices: 29.2 us -> 36.8 us  [shifted(): lax.ppermute(value, axis, [(src, fn(src) % size) for src in range(size)])]
    slice x0 -> x5, local copies, waits for them, and re-layouts: none -> 6.71 us  [the longest x2 3.53 us: body(): amp[sc_rows:]]
    all_gather x1, waiting for transfers between devices: 3.83 us -> 0.01 us  [body(): lax.all_gather(amp[:sc_rows], 'col', axis=1, tiled=True)]
    ppermute x8, starting transfers between devices: 19.2 us -> 15.8 us  [body(): flat = lax.ppermute(flat, ('row', 'col', 'slab'), pairs)]
    ppermute x17 -> x21, waiting for transfers between devices: 110 us -> 108 us  [shifted(): lax.ppermute(value, axis, [(src, fn(src) % size) for src in range(size)])]
  transfers between devices with their start and end apart: 26 -> 30, of which waited for: 14 -> 14; matrix products, arithmetic and copies ran while one was open for 15% -> 18% of each run, Pallas kernels for 0% -> 0%
where the time goes in v2:
time: 337 us; the launch traced here: 331 us
  waiting for transfers between devices  135 us (40%)
  local copies, waits for them, and re-layouts  81.8 us (24%)
  starting transfers between devices  52.5 us (16%)
  other arithmetic  23.2 us (7%)
  matrix products  21.8 us (6%)
  between operations  16.3 us (5%)
    ppermute x21, waiting for transfers between devices, shifted(): lax.ppermute(value, axis, [(src, fn(src) % size) for src in range(size)])  108 us
    ppermute x21, starting transfers between devices, shifted(): lax.ppermute(value, axis, [(src, fn(src) % size) for src in range(size)])  36.8 us
    ppermute x8, waiting for transfers between devices, body(): flat = lax.ppermute(flat, ('row', 'col', 'slab'), pairs)  27.3 us
    dot_general x2, matrix products, body(): jnp.einsum('ikca,kcjb->ijab', amp_part, int_abs, preferred_element_type=j...  21.8 us
    ppermute x8, starting transfers between devices, body(): flat = lax.ppermute(flat, ('row', 'col', 'slab'), pairs)  15.8 us
    reshape x2, local copies, waits for them, and re-layouts, body(): shares.reshape(i_n, j_n, a_n, n_slab, b_n // n_slab)  14.5 us
    transpose x1, local copies, waits for them, and re-layouts, body(): mirrored = jnp.transpose(gathered, (1, 2, 3, 0, 4)).reshape(shares.shape)  12.8 us
    select_n x1, other arithmetic, int_mask(): label_b = jnp.take(irreps, blocks + b_ids // VTILE)  11.8 us
  transfers between devices with their start and end apart: 30, of which 14 were waited for; matrix products, arithmetic and copies ran while one was open for 18% of the time, Pallas kernels for 0%

profile of v2, /device:TPU:0, one launch (start us, length us, event | category | flops | bytes accessed | tf_op | source)
XLA Modules:
  0.0 330.6 jit_solution(2495850962398103325)
XLA Ops:
  16.6 11.8 %and_select_fusion.1 = s32[128]{0:T(128)S(1)} fusion(s32[]{:T(128)} %bitcast.26, s32[]{:T(128)} %bitcast.27, s32[]{:T(128)} %bitcast.28, s32[]{:T(128)} %bitcast.29, s32[]{:T(128)} %bitcast.30, s32[]{:T(128)} %bitcast.32, s32[]{:T(128)} %bitcast.31, s32[]{:T(128)} %bitcast.3, s32[]{:T(128)} %bitcast.5, s32[]{:T(128)} %bitcast.7, s32[]{:T(128)} %bitcast.9, ...), kind=kLoop, calls=%fused_computation.100 | loop fusion | flops 8192 | bytes 588 | tf_op jit(solution)/shard_map/jit(_take)/select_n | solution.py:19
  39.5 44.2 %collective-permute-done.1 = bf16[12,60,12,128]{3,1,2,0:T(8,128)(2,1)} collective-permute-done((bf16[12,60,12,128]{3,1,2,0:T(8,128)(2,1)}, bf16[12,60,12,128]{3,1,2,0:T(8,128)(2,1)}, u32[]{:S(2)}, u32[]{:S(2)}) %collective-permute-start.1) | collective-permute-done | bytes 2211872 | tf_op jit(solution)/shard_map/ppermute | solution.py:12
  90.3 6.0 %broadcast_in_dim.38 = bf16[48,60,12,128]{3,1,0,2:T(8,128)(2,1)} broadcast(bf16[]{:T(256)} %constant.162.clone.1), dimensions={} | broadcast | bytes 8847362 | tf_op jit(solution)/shard_map/broadcast_in_dim | solution.py:29
  100.6 3.9 %collective-permute-done.12 = bf16[2,12,60,128]{3,2,1,0:T(8,128)(2,1)} collective-permute-done((bf16[2,12,60,128]{3,2,1,0:T(8,128)(2,1)S(1)}, bf16[2,12,60,128]{3,2,1,0:T(8,128)(2,1)}, u32[]{:S(2)}, u32[]{:S(2)}) %collective-permute-start.12) | collective-permute-done | bytes 368672 | tf_op jit(solution)/shard_map/ppermute | solution.py:12
  108.7 3.8 %copy_dynamic-update-slice_fusion.2 = bf16[48,60,12,128]{3,1,0,2:T(8,128)(2,1)} fusion(bf16[48,60,12,128]{3,1,0,2:T(8,128)(2,1)} %copy_dynamic-update-slice_fusion.3, s32[]{:T(128)S(6)} %select_n.285, bf16[12,60,12,128]{3,1,2,0:T(8,128)(2,1)} %collective-permute-done), kind=kLoop, calls=%fused_computation.11 | loop fusion | bytes 4718596 | tf_op jit(solution)/shard_map/dynamic_update_slice | solution.py:31
  112.4 3.8 %copy_dynamic-update-slice_fusion.1 = bf16[48,60,12,128]{3,1,0,2:T(8,128)(2,1)} fusion(bf16[48,60,12,128]{3,1,0,2:T(8,128)(2,1)} %copy_dynamic-update-slice_fusion.2, s32[]{:T(128)S(6)} %select_n.286, bf16[12,60,12,128]{3,1,2,0:T(8,128)(2,1)} %collective-permute-done.1), kind=kLoop, calls=%fused_computation.10 | loop fusion | bytes 4718596 | tf_op jit(solution)/shard_map/dynamic_update_slice | solution.py:31
  116.2 3.8 %copy_dynamic-update-slice_fusion = bf16[48,60,12,128]{3,1,0,2:T(8,128)(2,1)} fusion(bf16[48,60,12,128]{3,1,0,2:T(8,128)(2,1)} %copy_dynamic-update-slice_fusion.1, s32[]{:T(128)S(6)} %select_n.287, bf16[12,60,12,128]{3,1,2,0:T(8,128)(2,1)} %collective-permute-done.2), kind=kLoop, calls=%fused_computation.9 | loop fusion | bytes 4718596 | tf_op jit(solution)/shard_map/dynamic_update_slice | solution.py:31
  120.0 11.6 %fusion.7 = f32[6,12,128,128]{3,2,0,1:T(8,128)S(1)} fusion(bf16[8,48,60,128]{3,2,1,0:T(8,128)(2,1)} %all-gather.2.cloned.1.call-done, bf16[48,60,12,128]{3,1,0,2:T(8,128)(2,1)} %copy_dynamic-update-slice_fusion), kind=kOutput, calls=%fused_computation.15 | convolution fusion | flops 6794772480 | bytes 18874368 | tf_op jit(solution)/shard_map/ikca,kcjb->ijab/dot_general | solution.py:100
  135.4 10.2 %fusion.10 = f32[6,12,128,128]{3,2,0,1:T(8,128)S(1)} fusion(bf16[4,48,60,128]{3,2,1,0:T(8,128)(2,1)S(1)} %copy-done.4, bf16[8,48,60,128]{3,2,1,0:T(8,128)(2,1)S(1)} %copy-done.5, bf16[48,60,12,128]{3,1,0,2:T(8,128)(2,1)} %copy_dynamic-update-slice_fusion), kind=kOutput, calls=%fused_computation.16 | convolution fusion | flops 6803619840 | bytes 22413312 | tf_op jit(solution)/shard_map/ikca,kcjb->ijab/dot_general | solution.py:100
  149.5 3.3 collective-permute-start.7
  153.0 10.0 %collective-permute-done.17 = f32[6,6,32,128]{3,2,0,1:T(8,128)S(1)} collective-permute-done((f32[6,6,32,128]{3,2,0,1:T(8,128)S(1)}, f32[6,6,32,128]{3,2,0,1:T(8,128)S(1)}, u32[]{:S(2)}, u32[]{:S(2)}) %collective-permute-start.17) | collective-permute-done | bytes 589856 | tf_op jit(solution)/shard_map/ppermute | solution.py:12
  163.1 3.8 %collective-permute-start.18 = (f32[6,6,32,128]{3,2,0,1:T(8,128)S(1)}, f32[6,6,32,128]{3,2,0,1:T(8,128)S(1)}, u32[]{:S(2)}, u32[]{:S(2)}) collective-permute-start(f32[6,6,32,128]{3,2,0,1:T(8,128)S(1)} %dynamic-slice_add_fusion.2), channel_id=1, source_target_pairs={{0,6},{1,7},{2,0},{3,1},{4,2},{5,3},{6,4},{7,5},{8,14},{9,15},{10,... | collective-permute-start | bytes 1769480 | tf_op jit(solution)/shard_map/ppermute | solution.py:12
  167.0 8.6 %collective-permute-done.7 = f32[6,6,32,128]{3,2,0,1:T(8,128)S(1)} collective-permute-done((f32[6,6,32,128]{3,2,0,1:T(8,128)S(1)}, f32[6,6,32,128]{3,2,0,1:T(8,128)S(1)}, u32[]{:S(2)}, u32[]{:S(2)}) %collective-permute-start.7) | collective-permute-done | bytes 589856 | tf_op jit(solution)/shard_map/ppermute | solution.py:12
  175.7 3.8 %collective-permute-start.8 = (f32[6,6,32,128]{3,2,0,1:T(8,128)S(1)}, f32[6,6,32,128]{3,2,0,1:T(8,128)S(1)}, u32[]{:S(2)}, u32[]{:S(2)}) collective-permute-start(f32[6,6,32,128]{3,2,0,1:T(8,128)S(1)} %dynamic-slice_add_fusion.7), channel_id=1, source_target_pairs={{0,6},{1,7},{2,0},{3,1},{4,2},{5,3},{6,4},{7,5},{8,14},{9,15},{10,... | collective-permute-start | bytes 1769480 | tf_op jit(solution)/shard_map/ppermute | solution.py:12
  179.7 8.6 %collective-permute-done.18 = f32[6,6,32,128]{3,2,0,1:T(8,128)S(1)} collective-permute-done((f32[6,6,32,128]{3,2,0,1:T(8,128)S(1)}, f32[6,6,32,128]{3,2,0,1:T(8,128)S(1)}, u32[]{:S(2)}, u32[]{:S(2)}) %collective-permute-start.18) | collective-permute-done | bytes 589856 | tf_op jit(solution)/shard_map/ppermute | solution.py:12
  188.4 3.8 %collective-permute-start.19 = (f32[6,6,32,128]{3,2,0,1:T(8,128)S(1)}, f32[6,6,32,128]{3,2,0,1:T(8,128)S(1)}, u32[]{:S(2)}, u32[]{:S(2)}) collective-permute-start(f32[6,6,32,128]{3,2,0,1:T(8,128)S(1)} %dynamic-slice_add_fusion.1), channel_id=1, source_target_pairs={{0,6},{1,7},{2,0},{3,1},{4,2},{5,3},{6,4},{7,5},{8,14},{9,15},{10,... | collective-permute-start | bytes 1769480 | tf_op jit(solution)/shard_map/ppermute | solution.py:12
  192.3 8.6 %collective-permute-done.8 = f32[6,6,32,128]{3,2,0,1:T(8,128)S(1)} collective-permute-done((f32[6,6,32,128]{3,2,0,1:T(8,128)S(1)}, f32[6,6,32,128]{3,2,0,1:T(8,128)S(1)}, u32[]{:S(2)}, u32[]{:S(2)}) %collective-permute-start.8) | collective-permute-done | bytes 589856 | tf_op jit(solution)/shard_map/ppermute | solution.py:12
  201.0 3.7 %collective-permute-done.5 = f32[6,6,32,128]{3,2,0,1:T(8,128)S(1)} collective-permute-done((f32[6,6,32,128]{3,2,0,1:T(8,128)S(1)}, f32[6,6,32,128]{3,2,0,1:T(8,128)S(1)}, u32[]{:S(2)}, u32[]{:S(2)}) %collective-permute-start.5) | collective-permute-done | bytes 589856 | tf_op jit(solution)/shard_map/ppermute | solution.py:12
  208.1 3.8 %collective-permute-done.19 = f32[6,6,32,128]{3,2,0,1:T(8,128)S(1)} collective-permute-done((f32[6,6,32,128]{3,2,0,1:T(8,128)S(1)}, f32[6,6,32,128]{3,2,0,1:T(8,128)S(1)}, u32[]{:S(2)}, u32[]{:S(2)}) %collective-permute-start.19) | collective-permute-done | bytes 589856 | tf_op jit(solution)/shard_map/ppermute | solution.py:12
  212.0 3.4 %collective-permute-done.16 = f32[6,6,32,128]{3,2,0,1:T(8,128)S(1)} collective-permute-done((f32[6,6,32,128]{3,2,0,1:T(8,128)S(1)}, f32[6,6,32,128]{3,2,0,1:T(8,128)S(1)}, u32[]{:S(2)}, u32[]{:S(2)}) %collective-permute-start.16) | collective-permute-done | bytes 589856 | tf_op jit(solution)/shard_map/ppermute | solution.py:12
  216.4 3.4 %collective-permute-start.20 = (f32[6,12,16,128]{3,2,0,1:T(8,128)}, f32[6,12,16,128]{3,2,0,1:T(8,128)}, u32[]{:S(2)}, u32[]{:S(2)}) collective-permute-start(f32[6,12,16,128]{3,2,0,1:T(8,128)} %fusion.15), channel_id=1, source_target_pairs={{0,1},{1,0},{2,3},{3,2},{4,5},{5,4},{6,7},{7,6},{8,9},{9,8},{10,11... | collective-permute-start | bytes 1769480 | tf_op jit(solution)/shard_map/ppermute | solution.py:12
  219.9 12.0 %collective-permute-done.20 = f32[6,12,16,128]{3,2,0,1:T(8,128)} collective-permute-done((f32[6,12,16,128]{3,2,0,1:T(8,128)}, f32[6,12,16,128]{3,2,0,1:T(8,128)}, u32[]{:S(2)}, u32[]{:S(2)}) %collective-permute-start.20) | collective-permute-done | bytes 589856 | tf_op jit(solution)/shard_map/ppermute | solution.py:12
  233.2 4.9 %reshape.206 = f32[12,12,16,8,16]{4,3,2,0,1:T(8,128)} reshape(f32[12,12,16,128]{3,2,0,1:T(8,128)S(1)} %pad_maximum_fusion.1) | data formatting | bytes 2359296 | tf_op jit(solution)/shard_map/reshape | solution.py:111
  238.1 9.6 %copy.27 = f32[12,12,16,8,16]{2,4,0,1,3:T(8,128)} copy(f32[12,12,16,8,16]{4,3,2,0,1:T(8,128)} %reshape.206) | data formatting | bytes 2359296 | tf_op jit(solution)/shard_map/reshape | solution.py:111
  247.7 6.9 %reshape.207 = f32[8,144,256]{2,1,0:T(8,128)S(1)} reshape(f32[8,12,12,16,16]{4,3,2,1,0:T(8,128)} %bitcast.142) | data formatting | bytes 2359296 | tf_op jit(solution)/shard_map/reshape | solution.py:112
  260.7 5.9 %collective-permute-start.26 = (f32[1,144,256]{2,1,0:T(8,128)S(1)}, f32[1,144,256]{2,1,0:T(8,128)S(1)}, u32[]{:S(2)}, u32[]{:S(2)}) collective-permute-start(f32[1,144,256]{2,1,0:T(8,128)S(1)} %get-tuple-element.13), channel_id=1, source_target_pairs={{0,5},{1,4},{2,7},{3,6},{4,1},{5,0},{6,3},{7,2},{8,37},{9,36},{10,... | collective-permute-start | bytes 442376 | tf_op jit(solution)/shard_map/ppermute | solution.py:122
  270.6 10.0 %collective-permute-done.24 = f32[1,144,256]{2,1,0:T(8,128)S(1)} collective-permute-done((f32[1,144,256]{2,1,0:T(8,128)S(1)}, f32[1,144,256]{2,1,0:T(8,128)S(1)}, u32[]{:S(2)}, u32[]{:S(2)}) %collective-permute-start.24) | collective-permute-done | bytes 147488 | tf_op jit(solution)/shard_map/ppermute | solution.py:122
  280.6 13.7 %collective-permute-done.25 = f32[1,144,256]{2,1,0:T(8,128)S(1)} collective-permute-done((f32[1,144,256]{2,1,0:T(8,128)S(1)}, f32[1,144,256]{2,1,0:T(8,128)S(1)}, u32[]{:S(2)}, u32[]{:S(2)}) %collective-permute-start.25) | collective-permute-done | bytes 147488 | tf_op jit(solution)/shard_map/ppermute | solution.py:122
  294.3 3.6 %collective-permute-done.26 = f32[1,144,256]{2,1,0:T(8,128)S(1)} collective-permute-done((f32[1,144,256]{2,1,0:T(8,128)S(1)}, f32[1,144,256]{2,1,0:T(8,128)S(1)}, u32[]{:S(2)}, u32[]{:S(2)}) %collective-permute-start.26) | collective-permute-done | bytes 147488 | tf_op jit(solution)/shard_map/ppermute | solution.py:122
  298.1 5.1 %reshape.208 = f32[8,12,12,16,16]{4,3,2,1,0:T(8,128)} reshape(f32[8,144,256]{2,1,0:T(8,128)S(1)} %constant_dynamic-update-slice_fusion) | data formatting | bytes 2359296 | tf_op jit(solution)/shard_map/reshape | solution.py:124
  303.2 12.8 %copy.28 = f32[12,12,16,8,16]{4,3,2,0,1:T(8,128)} copy(f32[12,12,16,8,16]{4,2,1,0,3:T(8,128)} %bitcast.143) | data formatting | bytes 2359296 | tf_op jit(solution)/shard_map/transpose | solution.py:125
  315.9 6.2 %reshape.209 = f32[12,12,16,128]{3,2,0,1:T(8,128)S(1)} reshape(f32[12,12,16,8,16]{4,3,2,0,1:T(8,128)} %copy.28) | data formatting | bytes 2359296 | tf_op jit(solution)/shard_map/reshape | solution.py:125
  (111 shorter events, 59.9 us)
Async XLA Ops:
  6.5 113.5 %all-gather.2.cloned.1.call-start = ((), (), s32[]{:S(2)}) async-start(), calls=%async_computation | async-start | bytes 7864320 | tf_op jit(solution)/shard_map/all_gather | solution.py:87
  11.7 16.8 %copy-start.1 = (bf16[12,60,12,128]{3,1,2,0:T(8,128)(2,1)S(1)}, bf16[12,60,12,128]{3,1,2,0:T(8,128)(2,1)}, u32[]{:S(2)}) copy-start(bf16[12,60,12,128]{3,1,2,0:T(8,128)(2,1)} %param.5) | copy-start | bytes 6635524
  30.2 53.6 %collective-permute-start.1 = (bf16[12,60,12,128]{3,1,2,0:T(8,128)(2,1)}, bf16[12,60,12,128]{3,1,2,0:T(8,128)(2,1)}, u32[]{:S(2)}, u32[]{:S(2)}) collective-permute-start(bf16[12,60,12,128]{3,1,2,0:T(8,128)(2,1)} %broadcast_select_fusion.1), channel_id=1, source_target_pairs={{0,64},{32,96},{64,0},{96,32},{1,65},{33,97},{65,1},{97,33},{2,66}... | collective-permute-start | bytes 6635528 | tf_op jit(solution)/shard_map/ppermute | solution.py:12
  32.2 76.5 %collective-permute-start = (bf16[12,60,12,128]{3,1,2,0:T(8,128)(2,1)}, bf16[12,60,12,128]{3,1,2,0:T(8,128)(2,1)}, u32[]{:S(2)}, u32[]{:S(2)}) collective-permute-start(bf16[12,60,12,128]{3,1,2,0:T(8,128)(2,1)} %broadcast_select_fusion.1), channel_id=1, source_target_pairs={{0,32},{32,0},{64,96},{96,64},{1,33},{33,1},{65,97},{97,65},{2,34}... | collective-permute-start | bytes 6635528 | tf_op jit(solution)/shard_map/ppermute | solution.py:12
  36.5 47.2 %collective-permute-start.11 = (bf16[4,12,60,128]{3,0,2,1:T(4,128)(2,1)}, bf16[4,12,60,128]{3,0,2,1:T(4,128)(2,1)S(1)}, u32[]{:S(2)}, u32[]{:S(2)}) collective-permute-start(bf16[4,12,60,128]{3,0,2,1:T(4,128)(2,1)} %copy.21), channel_id=1, source_target_pairs={{0,24},{8,16},{16,8},{24,0},{1,25},{9,17},{17,9},{25,1},{2,26},{10... | collective-permute-start | bytes 2211848 | tf_op jit(solution)/shard_map/ppermute | solution.py:12
  39.3 46.4 %collective-permute-start.10 = (bf16[4,12,60,128]{3,0,2,1:T(4,128)(2,1)}, bf16[4,12,60,128]{3,0,2,1:T(4,128)(2,1)}, u32[]{:S(2)}, u32[]{:S(2)}) collective-permute-start(bf16[4,12,60,128]{3,0,2,1:T(4,128)(2,1)} %copy.21), channel_id=1, source_target_pairs={{0,8},{8,0},{16,24},{24,16},{1,9},{9,1},{17,25},{25,17},{2,10},{10... | collective-permute-start | bytes 2211848 | tf_op jit(solution)/shard_map/ppermute | solution.py:12
  83.8 32.5 %collective-permute-start.2 = (bf16[12,60,12,128]{3,1,2,0:T(8,128)(2,1)}, bf16[12,60,12,128]{3,1,2,0:T(8,128)(2,1)}, u32[]{:S(2)}, u32[]{:S(2)}) collective-permute-start(bf16[12,60,12,128]{3,1,2,0:T(8,128)(2,1)} %collective-permute-done.1), channel_id=1, source_target_pairs={{0,32},{32,0},{64,96},{96,64},{1,33},{33,1},{65,97},{97,65},{2,34}... | collective-permute-start | bytes 6635528 | tf_op jit(solution)/shard_map/ppermute | solution.py:12
  84.1 20.5 %collective-permute-start.12 = (bf16[2,12,60,128]{3,2,1,0:T(8,128)(2,1)S(1)}, bf16[2,12,60,128]{3,2,1,0:T(8,128)(2,1)}, u32[]{:S(2)}, u32[]{:S(2)}) collective-permute-start(bf16[2,12,60,128]{3,2,1,0:T(8,128)(2,1)S(1)} %copy.40), channel_id=1, source_target_pairs={{0,8},{8,0},{16,24},{24,16},{1,9},{9,1},{17,25},{25,17},{2,10},{10... | collective-permute-start | bytes 1105928 | tf_op jit(solution)/shard_map/ppermute | solution.py:12
  88.0 17.4 %collective-permute-start.13 = (bf16[2,12,60,128]{3,2,1,0:T(8,128)(2,1)}, bf16[2,12,60,128]{3,2,1,0:T(8,128)(2,1)}, u32[]{:S(2)}, u32[]{:S(2)}) collective-permute-start(bf16[2,12,60,128]{3,2,1,0:T(8,128)(2,1)} %copy.39), channel_id=1, source_target_pairs={{0,24},{8,16},{16,8},{24,0},{1,25},{9,17},{17,9},{25,1},{2,26},{10... | collective-permute-start | bytes 1105928 | tf_op jit(solution)/shard_map/ppermute | solution.py:12
  131.6 3.8 %copy-start.4 = (bf16[4,48,60,128]{3,2,1,0:T(8,128)(2,1)S(1)}, bf16[4,48,60,128]{3,2,1,0:T(8,128)(2,1)}, u32[]{:S(2)}) copy-start(bf16[4,48,60,128]{3,2,1,0:T(8,128)(2,1)} %constant_dynamic-update-slice_fusion.8) | copy-start | bytes 8847364
  132.2 17.1 %collective-permute-start.6 = (f32[6,6,32,128]{3,2,0,1:T(8,128)S(1)}, f32[6,6,32,128]{3,2,0,1:T(8,128)S(1)}, u32[]{:S(2)}, u32[]{:S(2)}) collective-permute-start(f32[6,6,32,128]{3,2,0,1:T(8,128)S(1)} %constant_dynamic-slice_fusion.10), channel_id=1, source_target_pairs={{0,6},{1,7},{2,0},{3,1},{4,2},{5,3},{6,4},{7,5},{8,14},{9,15},{10,... | collective-permute-start | bytes 1769480 | tf_op jit(solution)/shard_map/ppermute | solution.py:12
  135.1 17.7 %collective-permute-start.3 = (f32[6,6,32,128]{3,2,0,1:T(8,128)S(1)}, f32[6,6,32,128]{3,2,0,1:T(8,128)S(1)}, u32[]{:S(2)}, u32[]{:S(2)}) collective-permute-start(f32[6,6,32,128]{3,2,0,1:T(8,128)S(1)} %constant_dynamic-slice_fusion.11), channel_id=1, source_target_pairs={{0,2},{1,3},{2,4},{3,5},{4,6},{5,7},{6,0},{7,1},{8,10},{9,11},{10,... | collective-permute-start | bytes 1769480 | tf_op jit(solution)/shard_map/ppermute | solution.py:12
  146.0 17.0 %collective-permute-start.17 = (f32[6,6,32,128]{3,2,0,1:T(8,128)S(1)}, f32[6,6,32,128]{3,2,0,1:T(8,128)S(1)}, u32[]{:S(2)}, u32[]{:S(2)}) collective-permute-start(f32[6,6,32,128]{3,2,0,1:T(8,128)S(1)} %constant_dynamic-slice_fusion.8), channel_id=1, source_target_pairs={{0,6},{1,7},{2,0},{3,1},{4,2},{5,3},{6,4},{7,5},{8,14},{9,15},{10,... | collective-permute-start | bytes 1769480 | tf_op jit(solution)/shard_map/ppermute | solution.py:12
  149.3 17.5 %collective-permute-start.14 = (f32[6,6,32,128]{3,2,0,1:T(8,128)S(1)}, f32[6,6,32,128]{3,2,0,1:T(8,128)S(1)}, u32[]{:S(2)}, u32[]{:S(2)}) collective-permute-start(f32[6,6,32,128]{3,2,0,1:T(8,128)S(1)} %constant_dynamic-slice_fusion.9), channel_id=1, source_target_pairs={{0,2},{1,3},{2,4},{3,5},{4,6},{5,7},{6,0},{7,1},{8,10},{9,11},{10,... | collective-permute-start | bytes 1769480 | tf_op jit(solution)/shard_map/ppermute | solution.py:12
  149.5 26.1 %collective-permute-start.7 = (f32[6,6,32,128]{3,2,0,1:T(8,128)S(1)}, f32[6,6,32,128]{3,2,0,1:T(8,128)S(1)}, u32[]{:S(2)}, u32[]{:S(2)}) collective-permute-start(f32[6,6,32,128]{3,2,0,1:T(8,128)S(1)} %dynamic-slice_add_fusion.8), channel_id=1, source_target_pairs={{0,6},{1,7},{2,0},{3,1},{4,2},{5,3},{6,4},{7,5},{8,14},{9,15},{10,... | collective-permute-start | bytes 1769480 | tf_op jit(solution)/shard_map/ppermute | solution.py:12
  152.9 26.6 %collective-permute-start.4 = (f32[6,6,32,128]{3,2,0,1:T(8,128)S(1)}, f32[6,6,32,128]{3,2,0,1:T(8,128)S(1)}, u32[]{:S(2)}, u32[]{:S(2)}) collective-permute-start(f32[6,6,32,128]{3,2,0,1:T(8,128)S(1)} %dynamic-slice_add_fusion.11), channel_id=1, source_target_pairs={{0,2},{1,3},{2,4},{3,5},{4,6},{5,7},{6,0},{7,1},{8,10},{9,11},{10,... | collective-permute-start | bytes 1769480 | tf_op jit(solution)/shard_map/ppermute | solution.py:12
  163.1 25.2 %collective-permute-start.18 = (f32[6,6,32,128]{3,2,0,1:T(8,128)S(1)}, f32[6,6,32,128]{3,2,0,1:T(8,128)S(1)}, u32[]{:S(2)}, u32[]{:S(2)}) collective-permute-start(f32[6,6,32,128]{3,2,0,1:T(8,128)S(1)} %dynamic-slice_add_fusion.2), channel_id=1, source_target_pairs={{0,6},{1,7},{2,0},{3,1},{4,2},{5,3},{6,4},{7,5},{8,14},{9,15},{10,... | collective-permute-start | bytes 1769480 | tf_op jit(solution)/shard_map/ppermute | solution.py:12
  166.9 25.2 %collective-permute-start.15 = (f32[6,6,32,128]{3,2,0,1:T(8,128)S(1)}, f32[6,6,32,128]{3,2,0,1:T(8,128)S(1)}, u32[]{:S(2)}, u32[]{:S(2)}) collective-permute-start(f32[6,6,32,128]{3,2,0,1:T(8,128)S(1)} %dynamic-slice_add_fusion.5), channel_id=1, source_target_pairs={{0,2},{1,3},{2,4},{3,5},{4,6},{5,7},{6,0},{7,1},{8,10},{9,11},{10,... | collective-permute-start | bytes 1769480 | tf_op jit(solution)/shard_map/ppermute | solution.py:12
  175.7 25.2 %collective-permute-start.8 = (f32[6,6,32,128]{3,2,0,1:T(8,128)S(1)}, f32[6,6,32,128]{3,2,0,1:T(8,128)S(1)}, u32[]{:S(2)}, u32[]{:S(2)}) collective-permute-start(f32[6,6,32,128]{3,2,0,1:T(8,128)S(1)} %dynamic-slice_add_fusion.7), channel_id=1, source_target_pairs={{0,6},{1,7},{2,0},{3,1},{4,2},{5,3},{6,4},{7,5},{8,14},{9,15},{10,... | collective-permute-start | bytes 1769480 | tf_op jit(solution)/shard_map/ppermute | solution.py:12
  179.6 25.1 %collective-permute-start.5 = (f32[6,6,32,128]{3,2,0,1:T(8,128)S(1)}, f32[6,6,32,128]{3,2,0,1:T(8,128)S(1)}, u32[]{:S(2)}, u32[]{:S(2)}) collective-permute-start(f32[6,6,32,128]{3,2,0,1:T(8,128)S(1)} %dynamic-slice_add_fusion.10), channel_id=1, source_target_pairs={{0,2},{1,3},{2,4},{3,5},{4,6},{5,7},{6,0},{7,1},{8,10},{9,11},{10,... | collective-permute-start | bytes 1769480 | tf_op jit(solution)/shard_map/ppermute | solution.py:12
  188.4 23.6 %collective-permute-start.19 = (f32[6,6,32,128]{3,2,0,1:T(8,128)S(1)}, f32[6,6,32,128]{3,2,0,1:T(8,128)S(1)}, u32[]{:S(2)}, u32[]{:S(2)}) collective-permute-start(f32[6,6,32,128]{3,2,0,1:T(8,128)S(1)} %dynamic-slice_add_fusion.1), channel_id=1, source_target_pairs={{0,6},{1,7},{2,0},{3,1},{4,2},{5,3},{6,4},{7,5},{8,14},{9,15},{10,... | collective-permute-start | bytes 1769480 | tf_op jit(solution)/shard_map/ppermute | solution.py:12
  192.2 23.2 %collective-permute-start.16 = (f32[6,6,32,128]{3,2,0,1:T(8,128)S(1)}, f32[6,6,32,128]{3,2,0,1:T(8,128)S(1)}, u32[]{:S(2)}, u32[]{:S(2)}) collective-permute-start(f32[6,6,32,128]{3,2,0,1:T(8,128)S(1)} %dynamic-slice_add_fusion.4), channel_id=1, source_target_pairs={{0,2},{1,3},{2,4},{3,5},{4,6},{5,7},{6,0},{7,1},{8,10},{9,11},{10,... | collective-permute-start | bytes 1769480 | tf_op jit(solution)/shard_map/ppermute | solution.py:12
  204.9 14.9 %collective-permute-start.9 = (f32[6,12,16,128]{3,2,0,1:T(8,128)S(1)}, f32[6,12,16,128]{3,2,0,1:T(8,128)S(1)}, u32[]{:S(2)}, u32[]{:S(2)}) collective-permute-start(f32[6,12,16,128]{3,2,0,1:T(8,128)S(1)} %fusion.18), channel_id=1, source_target_pairs={{0,1},{1,0},{2,3},{3,2},{4,5},{5,4},{6,7},{7,6},{8,9},{9,8},{10,11... | collective-permute-start | bytes 1769480 | tf_op jit(solution)/shard_map/ppermute | solution.py:12
  216.4 15.5 %collective-permute-start.20 = (f32[6,12,16,128]{3,2,0,1:T(8,128)}, f32[6,12,16,128]{3,2,0,1:T(8,128)}, u32[]{:S(2)}, u32[]{:S(2)}) collective-permute-start(f32[6,12,16,128]{3,2,0,1:T(8,128)} %fusion.15), channel_id=1, source_target_pairs={{0,1},{1,0},{2,3},{3,2},{4,5},{5,4},{6,7},{7,6},{8,9},{9,8},{10,11... | collective-permute-start | bytes 1769480 | tf_op jit(solution)/shard_map/ppermute | solution.py:12
  254.7 6.0 %collective-permute-start.21 = (f32[1,144,256]{2,1,0:T(8,128)S(1)}, f32[1,144,256]{2,1,0:T(8,128)S(1)}, u32[]{:S(2)}, u32[]{:S(2)}) collective-permute-start(f32[1,144,256]{2,1,0:T(8,128)S(1)} %get-tuple-element.18), channel_id=1, source_target_pairs={{0,0},{1,1},{2,2},{3,3},{4,4},{5,5},{6,6},{7,7},{8,32},{9,33},{10,... | collective-permute-start | bytes 442376 | tf_op jit(solution)/shard_map/ppermute | solution.py:122
  255.4 11.4 %collective-permute-start.22 = (f32[1,144,256]{2,1,0:T(8,128)S(1)}, f32[1,144,256]{2,1,0:T(8,128)S(1)}, u32[]{:S(2)}, u32[]{:S(2)}) collective-permute-start(f32[1,144,256]{2,1,0:T(8,128)S(1)} %get-tuple-element.17), channel_id=1, source_target_pairs={{0,1},{1,0},{2,3},{3,2},{4,5},{5,4},{6,7},{7,6},{8,33},{9,32},{10,... | collective-permute-start | bytes 442376 | tf_op jit(solution)/shard_map/ppermute | solution.py:122
  258.6 8.8 %collective-permute-start.23 = (f32[1,144,256]{2,1,0:T(8,128)S(1)}, f32[1,144,256]{2,1,0:T(8,128)S(1)}, u32[]{:S(2)}, u32[]{:S(2)}) collective-permute-start(f32[1,144,256]{2,1,0:T(8,128)S(1)} %get-tuple-element.16), channel_id=1, source_target_pairs={{0,2},{1,3},{2,0},{3,1},{4,6},{5,7},{6,4},{7,5},{8,34},{9,35},{10,... | collective-permute-start | bytes 442376 | tf_op jit(solution)/shard_map/ppermute | solution.py:122
  258.6 22.0 %collective-permute-start.24 = (f32[1,144,256]{2,1,0:T(8,128)S(1)}, f32[1,144,256]{2,1,0:T(8,128)S(1)}, u32[]{:S(2)}, u32[]{:S(2)}) collective-permute-start(f32[1,144,256]{2,1,0:T(8,128)S(1)} %get-tuple-element.15), channel_id=1, source_target_pairs={{0,3},{1,2},{2,1},{3,0},{4,7},{5,6},{6,5},{7,4},{8,35},{9,34},{10,... | collective-permute-start | bytes 442376 | tf_op jit(solution)/shard_map/ppermute | solution.py:122
  260.4 33.9 %collective-permute-start.25 = (f32[1,144,256]{2,1,0:T(8,128)S(1)}, f32[1,144,256]{2,1,0:T(8,128)S(1)}, u32[]{:S(2)}, u32[]{:S(2)}) collective-permute-start(f32[1,144,256]{2,1,0:T(8,128)S(1)} %get-tuple-element.14), channel_id=1, source_target_pairs={{0,4},{1,5},{2,6},{3,7},{4,0},{5,1},{6,2},{7,3},{8,36},{9,37},{10,... | collective-permute-start | bytes 442376 | tf_op jit(solution)/shard_map/ppermute | solution.py:122
  260.7 37.3 %collective-permute-start.26 = (f32[1,144,256]{2,1,0:T(8,128)S(1)}, f32[1,144,256]{2,1,0:T(8,128)S(1)}, u32[]{:S(2)}, u32[]{:S(2)}) collective-permute-start(f32[1,144,256]{2,1,0:T(8,128)S(1)} %get-tuple-element.13), channel_id=1, source_target_pairs={{0,5},{1,4},{2,7},{3,6},{4,1},{5,0},{6,3},{7,2},{8,37},{9,36},{10,... | collective-permute-start | bytes 442376 | tf_op jit(solution)/shard_map/ppermute | solution.py:122
  266.7 31.3 %collective-permute-start.27 = (f32[1,144,256]{2,1,0:T(8,128)S(1)}, f32[1,144,256]{2,1,0:T(8,128)S(1)}, u32[]{:S(2)}, u32[]{:S(2)}) collective-permute-start(f32[1,144,256]{2,1,0:T(8,128)S(1)} %get-tuple-element.12), channel_id=1, source_target_pairs={{0,6},{1,7},{2,4},{3,5},{4,2},{5,3},{6,0},{7,1},{8,38},{9,39},{10,... | collective-permute-start | bytes 442376 | tf_op jit(solution)/shard_map/ppermute | solution.py:122
  267.4 30.6 %collective-permute-start.28 = (f32[1,144,256]{2,1,0:T(8,128)S(1)}, f32[1,144,256]{2,1,0:T(8,128)S(1)}, u32[]{:S(2)}, u32[]{:S(2)}) collective-permute-start(f32[1,144,256]{2,1,0:T(8,128)S(1)} %get-tuple-element.11), channel_id=1, source_target_pairs={{0,7},{1,6},{2,5},{3,4},{4,3},{5,2},{6,1},{7,0},{8,39},{9,38},{10,... | collective-permute-start | bytes 442376 | tf_op jit(solution)/shard_map/ppermute | solution.py:122
  (4 other events, 8.6 us)
Sparse Core Ops, SparseCore 0:
  13.3 92.0 all-gather.1

commit v3 on v0

--- a/solution.py
+++ b/solution.py
@@ -71,7 +71,7 @@
     int_abs = gather_row(ints, row_at)
     n_row = lax.axis_size("row")
     n_col = lax.axis_size("col")
-    n_chunks = 2
+    n_chunks = 3
     rows = i_rows // n_chunks
     share_parts = []
     for ch in range(n_chunks):

time: 319 us -> 317 us (level)
  matrix products: 21.7 us -> 25.6 us
  other arithmetic: 22.4 us -> 19.1 us
    dot_general x2 -> x3, matrix products: 21.7 us -> 25.6 us  [body(): jnp.einsum('ikca,kcjb->ijab', amp_part, int_abs, preferred_element_type=j...]
    ppermute x17 -> x24, waiting for transfers between devices: 110 us -> 106 us  [shifted(): lax.ppermute(value, axis, [(src, fn(src) % size) for src in range(size)])]
    ppermute x17 -> x24, starting transfers between devices: 29.2 us -> 30.2 us  [shifted(): lax.ppermute(value, axis, [(src, fn(src) % size) for src in range(size)])]
  transfers between devices with their start and end apart: 26 -> 33, of which waited for: 14 -> 21; matrix products, arithmetic and copies ran while one was open for 15% -> 17% of each run, Pallas kernels for 0% -> 0%
where the time goes in v3:
time: 317 us; the launch traced here: 316 us
  waiting for transfers between devices  137 us (43%)
  local copies, waits for them, and re-layouts  69.2 us (22%)
  starting transfers between devices  49.1 us (15%)
  matrix products  25.6 us (8%)
  other arithmetic  19.1 us (6%)
  between operations  15.8 us (5%)
    ppermute x24, waiting for transfers between devices, shifted(): lax.ppermute(value, axis, [(src, fn(src) % size) for src in range(size)])  106 us
    ppermute x24, starting transfers between devices, shifted(): lax.ppermute(value, axis, [(src, fn(src) % size) for src in range(size)])  30.2 us
    ppermute x8, waiting for transfers between devices, body(): flat = lax.ppermute(flat, ('row', 'col', 'slab'), pairs)  27 us
    dot_general x3, matrix products, body(): jnp.einsum('ikca,kcjb->ijab', amp_part, int_abs, preferred_element_type=j...  25.6 us
    ppermute x8, starting transfers between devices, body(): flat = lax.ppermute(flat, ('row', 'col', 'slab'), pairs)  18.9 us
    reshape x2, local copies, waits for them, and re-layouts, body(): shares.reshape(i_n, j_n, a_n, n_slab, b_n // n_slab)  14.5 us
    transpose x1, local copies, waits for them, and re-layouts, body(): mirrored = jnp.transpose(gathered, (1, 2, 3, 0, 4)).reshape(shares.shape)  12.8 us
    select_n x1, other arithmetic, int_mask(): label_b = jnp.take(irreps, blocks + b_ids // VTILE)  11.9 us
  transfers between devices with their start and end apart: 33, of which 21 were waited for; matrix products, arithmetic and copies ran while one was open for 17% of the time, Pallas kernels for 0%

profile of v3, /device:TPU:0, one launch (start us, length us, event | category | flops | bytes accessed | tf_op | source)
XLA Modules:
  0.0 316.1 jit_solution(16022020202664988851)
XLA Ops:
  14.1 11.9 %and_select_fusion.1 = s32[128]{0:T(128)S(1)} fusion(s32[]{:T(128)} %bitcast.26, s32[]{:T(128)} %bitcast.27, s32[]{:T(128)} %bitcast.28, s32[]{:T(128)} %bitcast.29, s32[]{:T(128)} %bitcast.30, s32[]{:T(128)} %bitcast.32, s32[]{:T(128)} %bitcast.31, s32[]{:T(128)} %bitcast.3, s32[]{:T(128)} %bitcast.5, s32[]{:T(128)} %bitcast.7, s32[]{:T(128)} %bitcast.9, ...), kind=kLoop, calls=%fused_computation.113 | loop fusion | flops 8192 | bytes 588 | tf_op jit(solution)/shard_map/jit(_take)/select_n | solution.py:19
  27.7 3.7 %collective-permute-start.1 = (bf16[12,60,12,128]{3,1,2,0:T(8,128)(2,1)}, bf16[12,60,12,128]{3,1,2,0:T(8,128)(2,1)}, u32[]{:S(2)}, u32[]{:S(2)}) collective-permute-start(bf16[12,60,12,128]{3,1,2,0:T(8,128)(2,1)} %broadcast_select_fusion.1), channel_id=1, source_target_pairs={{0,64},{32,96},{64,0},{96,32},{1,65},{33,97},{65,1},{97,33},{2,66}... | collective-permute-start | bytes 6635528 | tf_op jit(solution)/shard_map/ppermute | solution.py:12
  31.4 51.6 %collective-permute-done.1 = bf16[12,60,12,128]{3,1,2,0:T(8,128)(2,1)} collective-permute-done((bf16[12,60,12,128]{3,1,2,0:T(8,128)(2,1)}, bf16[12,60,12,128]{3,1,2,0:T(8,128)(2,1)}, u32[]{:S(2)}, u32[]{:S(2)}) %collective-permute-start.1) | collective-permute-done | bytes 2211872 | tf_op jit(solution)/shard_map/ppermute | solution.py:12
  82.9 6.0 %broadcast_in_dim.35 = bf16[48,60,12,128]{3,1,0,2:T(8,128)(2,1)} broadcast(bf16[]{:T(256)} %constant.177.clone.1), dimensions={} | broadcast | bytes 8847362 | tf_op jit(solution)/shard_map/broadcast_in_dim | solution.py:29
  91.2 3.8 %copy_dynamic-update-slice_fusion.2 = bf16[48,60,12,128]{3,1,0,2:T(8,128)(2,1)} fusion(bf16[48,60,12,128]{3,1,0,2:T(8,128)(2,1)} %copy_dynamic-update-slice_fusion.3, s32[]{:T(128)S(6)} %select_n.298, bf16[12,60,12,128]{3,1,2,0:T(8,128)(2,1)} %collective-permute-done), kind=kLoop, calls=%fused_computation.12 | loop fusion | bytes 4718596 | tf_op jit(solution)/shard_map/dynamic_update_slice | solution.py:31
  95.0 3.8 %copy_dynamic-update-slice_fusion.1 = bf16[48,60,12,128]{3,1,0,2:T(8,128)(2,1)} fusion(bf16[48,60,12,128]{3,1,0,2:T(8,128)(2,1)} %copy_dynamic-update-slice_fusion.2, s32[]{:T(128)S(6)} %select_n.299, bf16[12,60,12,128]{3,1,2,0:T(8,128)(2,1)} %collective-permute-done.1), kind=kLoop, calls=%fused_computation.11 | loop fusion | bytes 4718596 | tf_op jit(solution)/shard_map/dynamic_update_slice | solution.py:31
  98.7 3.8 %copy_dynamic-update-slice_fusion = bf16[48,60,12,128]{3,1,0,2:T(8,128)(2,1)} fusion(bf16[48,60,12,128]{3,1,0,2:T(8,128)(2,1)} %copy_dynamic-update-slice_fusion.1, s32[]{:T(128)S(6)} %select_n.300, bf16[12,60,12,128]{3,1,2,0:T(8,128)(2,1)} %collective-permute-done.2), kind=kLoop, calls=%fused_computation.10 | loop fusion | bytes 4718596 | tf_op jit(solution)/shard_map/dynamic_update_slice | solution.py:31
  102.5 3.8 %all-gather.2.cloned.1.call-done = bf16[12,48,60,128]{3,2,1,0:T(8,128)(2,1)} async-done(((bf16[12,12,60,128]{3,2,1,0:T(8,128)(2,1)}), bf16[12,48,60,128]{3,2,1,0:T(8,128)(2,1)}) %all-gather.2.cloned.1.call-update) | async-done | bytes 8847376 | tf_op jit(solution)/shard_map/all_gather | solution.py:70
  106.3 9.8 %fusion.6 = f32[4,12,128,128]{3,2,0,1:T(8,128)S(1)} fusion(bf16[12,48,60,128]{3,2,1,0:T(8,128)(2,1)} %all-gather.2.cloned.1.call-done, bf16[48,60,12,128]{3,1,0,2:T(8,128)(2,1)} %copy_dynamic-update-slice_fusion), kind=kOutput, calls=%fused_computation.16 | convolution fusion | flops 4529848320 | bytes 15728640 | tf_op jit(solution)/shard_map/ikca,kcjb->ijab/dot_general | solution.py:79
  119.7 7.9 %fusion.9 = f32[4,12,128,128]{3,2,0,1:T(8,128)S(1)} fusion(bf16[12,48,60,128]{3,2,1,0:T(8,128)(2,1)S(1)} %copy-done.2, bf16[48,60,12,128]{3,1,0,2:T(8,128)(2,1)} %copy_dynamic-update-slice_fusion), kind=kOutput, calls=%fused_computation.17 | convolution fusion | flops 4529848320 | bytes 15138816 | tf_op jit(solution)/shard_map/ikca,kcjb->ijab/dot_general | solution.py:79
  131.3 7.9 %fusion.12 = f32[4,12,128,128]{3,2,0,1:T(8,128)S(1)} fusion(bf16[12,48,60,128]{3,2,1,0:T(8,128)(2,1)S(1)} %copy-done.2, bf16[48,60,12,128]{3,1,0,2:T(8,128)(2,1)} %copy_dynamic-update-slice_fusion), kind=kOutput, calls=%fused_computation.18 | convolution fusion | flops 4529848320 | bytes 15138816 | tf_op jit(solution)/shard_map/ikca,kcjb->ijab/dot_general | solution.py:79
  152.3 3.7 %collective-permute-done.17 = f32[4,6,32,128]{3,2,0,1:T(8,128)S(1)} collective-permute-done((f32[4,6,32,128]{3,2,0,1:T(8,128)S(1)}, f32[4,6,32,128]{3,2,0,1:T(8,128)S(1)}, u32[]{:S(2)}, u32[]{:S(2)}) %collective-permute-start.17) | collective-permute-done | bytes 393248 | tf_op jit(solution)/shard_map/ppermute | solution.py:12
  156.2 4.5 %collective-permute-done.7 = f32[4,6,32,128]{3,2,0,1:T(8,128)S(1)} collective-permute-done((f32[4,6,32,128]{3,2,0,1:T(8,128)S(1)}, f32[4,6,32,128]{3,2,0,1:T(8,128)S(1)}, u32[]{:S(2)}, u32[]{:S(2)}) %collective-permute-start.7) | collective-permute-done | bytes 393248 | tf_op jit(solution)/shard_map/ppermute | solution.py:12
  160.8 3.7 %collective-permute-done.4 = f32[4,6,32,128]{3,2,0,1:T(8,128)S(1)} collective-permute-done((f32[4,6,32,128]{3,2,0,1:T(8,128)S(1)}, f32[4,6,32,128]{3,2,0,1:T(8,128)S(1)}, u32[]{:S(2)}, u32[]{:S(2)}) %collective-permute-start.4) | collective-permute-done | bytes 393248 | tf_op jit(solution)/shard_map/ppermute | solution.py:12
  164.6 4.5 %collective-permute-done.14 = f32[4,6,32,128]{3,2,0,1:T(8,128)S(1)} collective-permute-done((f32[4,6,32,128]{3,2,0,1:T(8,128)S(1)}, f32[4,6,32,128]{3,2,0,1:T(8,128)S(1)}, u32[]{:S(2)}, u32[]{:S(2)}) %collective-permute-start.14) | collective-permute-done | bytes 393248 | tf_op jit(solution)/shard_map/ppermute | solution.py:12
  169.2 3.7 %collective-permute-done.11 = f32[4,6,32,128]{3,2,0,1:T(8,128)S(1)} collective-permute-done((f32[4,6,32,128]{3,2,0,1:T(8,128)S(1)}, f32[4,6,32,128]{3,2,0,1:T(8,128)S(1)}, u32[]{:S(2)}, u32[]{:S(2)}) %collective-permute-start.11) | collective-permute-done | bytes 393248 | tf_op jit(solution)/shard_map/ppermute | solution.py:12
  173.0 4.5 %collective-permute-done.21 = f32[4,6,32,128]{3,2,0,1:T(8,128)S(1)} collective-permute-done((f32[4,6,32,128]{3,2,0,1:T(8,128)S(1)}, f32[4,6,32,128]{3,2,0,1:T(8,128)S(1)}, u32[]{:S(2)}, u32[]{:S(2)}) %collective-permute-start.21) | collective-permute-done | bytes 393248 | tf_op jit(solution)/shard_map/ppermute | solution.py:12
  177.6 3.7 %collective-permute-done.18 = f32[4,6,32,128]{3,2,0,1:T(8,128)S(1)} collective-permute-done((f32[4,6,32,128]{3,2,0,1:T(8,128)S(1)}, f32[4,6,32,128]{3,2,0,1:T(8,128)S(1)}, u32[]{:S(2)}, u32[]{:S(2)}) %collective-permute-start.18) | collective-permute-done | bytes 393248 | tf_op jit(solution)/shard_map/ppermute | solution.py:12
  181.7 4.3 %collective-permute-done.8 = f32[4,6,32,128]{3,2,0,1:T(8,128)S(1)} collective-permute-done((f32[4,6,32,128]{3,2,0,1:T(8,128)S(1)}, f32[4,6,32,128]{3,2,0,1:T(8,128)S(1)}, u32[]{:S(2)}, u32[]{:S(2)}) %collective-permute-start.8) | collective-permute-done | bytes 393248 | tf_op jit(solution)/shard_map/ppermute | solution.py:12
  186.0 3.7 %collective-permute-done.5 = f32[4,6,32,128]{3,2,0,1:T(8,128)S(1)} collective-permute-done((f32[4,6,32,128]{3,2,0,1:T(8,128)S(1)}, f32[4,6,32,128]{3,2,0,1:T(8,128)S(1)}, u32[]{:S(2)}, u32[]{:S(2)}) %collective-permute-start.5) | collective-permute-done | bytes 393248 | tf_op jit(solution)/shard_map/ppermute | solution.py:12
  194.5 3.7 %collective-permute-done.12 = f32[4,6,32,128]{3,2,0,1:T(8,128)S(1)} collective-permute-done((f32[4,6,32,128]{3,2,0,1:T(8,128)S(1)}, f32[4,6,32,128]{3,2,0,1:T(8,128)S(1)}, u32[]{:S(2)}, u32[]{:S(2)}) %collective-permute-start.12) | collective-permute-done | bytes 393248 | tf_op jit(solution)/shard_map/ppermute | solution.py:12
  209.8 6.3 %collective-permute-done.23 = f32[4,12,16,128]{3,2,0,1:T(8,128)S(1)} collective-permute-done((f32[4,12,16,128]{3,2,0,1:T(8,128)S(1)}, f32[4,12,16,128]{3,2,0,1:T(8,128)S(1)}, u32[]{:S(2)}, u32[]{:S(2)}) %collective-permute-start.23) | collective-permute-done | bytes 393248 | tf_op jit(solution)/shard_map/ppermute | solution.py:12
  216.3 4.9 %reshape.206 = f32[12,12,16,8,16]{4,3,2,0,1:T(8,128)} reshape(f32[12,12,16,128]{3,2,0,1:T(8,128)S(1)} %pad_maximum_fusion) | data formatting | bytes 2359296 | tf_op jit(solution)/shard_map/reshape | solution.py:90
  221.2 9.6 %copy.14 = f32[12,12,16,8,16]{2,4,0,1,3:T(8,128)} copy(f32[12,12,16,8,16]{4,3,2,0,1:T(8,128)} %reshape.206) | data formatting | bytes 2359296 | tf_op jit(solution)/shard_map/reshape | solution.py:90
  230.8 6.9 %reshape.207 = f32[8,144,256]{2,1,0:T(8,128)S(1)} reshape(f32[8,12,12,16,16]{4,3,2,1,0:T(8,128)} %bitcast.156) | data formatting | bytes 2359296 | tf_op jit(solution)/shard_map/reshape | solution.py:91
  244.9 4.7 %collective-permute-start.29 = (f32[1,144,256]{2,1,0:T(8,128)S(1)}, f32[1,144,256]{2,1,0:T(8,128)S(1)}, u32[]{:S(2)}, u32[]{:S(2)}) collective-permute-start(f32[1,144,256]{2,1,0:T(8,128)S(1)} %get-tuple-element.13), channel_id=1, source_target_pairs={{0,5},{1,4},{2,7},{3,6},{4,1},{5,0},{6,3},{7,2},{8,37},{9,36},{10,... | collective-permute-start | bytes 442376 | tf_op jit(solution)/shard_map/ppermute | solution.py:101
  252.9 7.1 %collective-permute-start.31 = (f32[1,144,256]{2,1,0:T(8,128)S(1)}, f32[1,144,256]{2,1,0:T(8,128)S(1)}, u32[]{:S(2)}, u32[]{:S(2)}) collective-permute-start(f32[1,144,256]{2,1,0:T(8,128)S(1)} %get-tuple-element.11), channel_id=1, source_target_pairs={{0,7},{1,6},{2,5},{3,4},{4,3},{5,2},{6,1},{7,0},{8,39},{9,38},{10,... | collective-permute-start | bytes 442376 | tf_op jit(solution)/shard_map/ppermute | solution.py:101
  259.9 4.4 %collective-permute-done.27 = f32[1,144,256]{2,1,0:T(8,128)S(1)} collective-permute-done((f32[1,144,256]{2,1,0:T(8,128)S(1)}, f32[1,144,256]{2,1,0:T(8,128)S(1)}, u32[]{:S(2)}, u32[]{:S(2)}) %collective-permute-start.27) | collective-permute-done | bytes 147488 | tf_op jit(solution)/shard_map/ppermute | solution.py:101
  264.4 16.7 %collective-permute-done.29 = f32[1,144,256]{2,1,0:T(8,128)S(1)} collective-permute-done((f32[1,144,256]{2,1,0:T(8,128)S(1)}, f32[1,144,256]{2,1,0:T(8,128)S(1)}, u32[]{:S(2)}, u32[]{:S(2)}) %collective-permute-start.29) | collective-permute-done | bytes 147488 | tf_op jit(solution)/shard_map/ppermute | solution.py:101
  284.0 5.1 %reshape.208 = f32[8,12,12,16,16]{4,3,2,1,0:T(8,128)} reshape(f32[8,144,256]{2,1,0:T(8,128)S(1)} %constant_dynamic-update-slice_fusion) | data formatting | bytes 2359296 | tf_op jit(solution)/shard_map/reshape | solution.py:103
  289.1 12.8 %copy.15 = f32[12,12,16,8,16]{4,3,2,0,1:T(8,128)} copy(f32[12,12,16,8,16]{4,2,1,0,3:T(8,128)} %bitcast.157) | data formatting | bytes 2359296 | tf_op jit(solution)/shard_map/transpose | solution.py:104
  301.9 6.2 %reshape.209 = f32[12,12,16,128]{3,2,0,1:T(8,128)S(1)} reshape(f32[12,12,16,8,16]{4,3,2,0,1:T(8,128)} %copy.15) | data formatting | bytes 2359296 | tf_op jit(solution)/shard_map/reshape | solution.py:104
  (112 shorter events, 61.5 us)
Async XLA Ops:
  6.5 99.8 %all-gather.2.cloned.1.call-start = ((), (), s32[]{:S(2)}) async-start(), calls=%async_computation | async-start | bytes 11796480 | tf_op jit(solution)/shard_map/all_gather | solution.py:70
  27.7 55.2 %collective-permute-start.1 = (bf16[12,60,12,128]{3,1,2,0:T(8,128)(2,1)}, bf16[12,60,12,128]{3,1,2,0:T(8,128)(2,1)}, u32[]{:S(2)}, u32[]{:S(2)}) collective-permute-start(bf16[12,60,12,128]{3,1,2,0:T(8,128)(2,1)} %broadcast_select_fusion.1), channel_id=1, source_target_pairs={{0,64},{32,96},{64,0},{96,32},{1,65},{33,97},{65,1},{97,33},{2,66}... | collective-permute-start | bytes 6635528 | tf_op jit(solution)/shard_map/ppermute | solution.py:12
  31.4 59.8 %collective-permute-start = (bf16[12,60,12,128]{3,1,2,0:T(8,128)(2,1)}, bf16[12,60,12,128]{3,1,2,0:T(8,128)(2,1)}, u32[]{:S(2)}, u32[]{:S(2)}) collective-permute-start(bf16[12,60,12,128]{3,1,2,0:T(8,128)(2,1)} %broadcast_select_fusion.1), channel_id=1, source_target_pairs={{0,32},{32,0},{64,96},{96,64},{1,33},{33,1},{65,97},{97,65},{2,34}... | collective-permute-start | bytes 6635528 | tf_op jit(solution)/shard_map/ppermute | solution.py:12
  82.9 15.8 %collective-permute-start.2 = (bf16[12,60,12,128]{3,1,2,0:T(8,128)(2,1)}, bf16[12,60,12,128]{3,1,2,0:T(8,128)(2,1)}, u32[]{:S(2)}, u32[]{:S(2)}) collective-permute-start(bf16[12,60,12,128]{3,1,2,0:T(8,128)(2,1)} %collective-permute-done.1), channel_id=1, source_target_pairs={{0,32},{32,0},{64,96},{96,64},{1,33},{33,1},{65,97},{97,65},{2,34}... | collective-permute-start | bytes 6635528 | tf_op jit(solution)/shard_map/ppermute | solution.py:12
  116.5 26.2 %collective-permute-start.6 = (f32[4,6,32,128]{3,2,0,1:T(8,128)S(1)}, f32[4,6,32,128]{3,2,0,1:T(8,128)S(1)}, u32[]{:S(2)}, u32[]{:S(2)}) collective-permute-start(f32[4,6,32,128]{3,2,0,1:T(8,128)S(1)} %constant_dynamic-slice_fusion.12), channel_id=1, source_target_pairs={{0,6},{1,7},{2,0},{3,1},{4,2},{5,3},{6,4},{7,5},{8,14},{9,15},{10,... | collective-permute-start | bytes 1179656 | tf_op jit(solution)/shard_map/ppermute | solution.py:12
  119.4 23.6 %collective-permute-start.3 = (f32[4,6,32,128]{3,2,0,1:T(8,128)S(1)}, f32[4,6,32,128]{3,2,0,1:T(8,128)S(1)}, u32[]{:S(2)}, u32[]{:S(2)}) collective-permute-start(f32[4,6,32,128]{3,2,0,1:T(8,128)S(1)} %constant_dynamic-slice_fusion.13), channel_id=1, source_target_pairs={{0,2},{1,3},{2,4},{3,5},{4,6},{5,7},{6,0},{7,1},{8,10},{9,11},{10,... | collective-permute-start | bytes 1179656 | tf_op jit(solution)/shard_map/ppermute | solution.py:12
  127.9 18.4 %collective-permute-start.13 = (f32[4,6,32,128]{3,2,0,1:T(8,128)S(1)}, f32[4,6,32,128]{3,2,0,1:T(8,128)S(1)}, u32[]{:S(2)}, u32[]{:S(2)}) collective-permute-start(f32[4,6,32,128]{3,2,0,1:T(8,128)S(1)} %constant_dynamic-slice_fusion.10), channel_id=1, source_target_pairs={{0,6},{1,7},{2,0},{3,1},{4,2},{5,3},{6,4},{7,5},{8,14},{9,15},{10,... | collective-permute-start | bytes 1179656 | tf_op jit(solution)/shard_map/ppermute | solution.py:12
  131.2 15.2 %collective-permute-start.10 = (f32[4,6,32,128]{3,2,0,1:T(8,128)S(1)}, f32[4,6,32,128]{3,2,0,1:T(8,128)S(1)}, u32[]{:S(2)}, u32[]{:S(2)}) collective-permute-start(f32[4,6,32,128]{3,2,0,1:T(8,128)S(1)} %constant_dynamic-slice_fusion.11), channel_id=1, source_target_pairs={{0,2},{1,3},{2,4},{3,5},{4,6},{5,7},{6,0},{7,1},{8,10},{9,11},{10,... | collective-permute-start | bytes 1179656 | tf_op jit(solution)/shard_map/ppermute | solution.py:12
  139.5 12.8 %collective-permute-start.20 = (f32[4,6,32,128]{3,2,0,1:T(8,128)S(1)}, f32[4,6,32,128]{3,2,0,1:T(8,128)S(1)}, u32[]{:S(2)}, u32[]{:S(2)}) collective-permute-start(f32[4,6,32,128]{3,2,0,1:T(8,128)S(1)} %constant_dynamic-slice_fusion.8), channel_id=1, source_target_pairs={{0,6},{1,7},{2,0},{3,1},{4,2},{5,3},{6,4},{7,5},{8,14},{9,15},{10,... | collective-permute-start | bytes 1179656 | tf_op jit(solution)/shard_map/ppermute | solution.py:12
  142.8 13.3 %collective-permute-start.17 = (f32[4,6,32,128]{3,2,0,1:T(8,128)S(1)}, f32[4,6,32,128]{3,2,0,1:T(8,128)S(1)}, u32[]{:S(2)}, u32[]{:S(2)}) collective-permute-start(f32[4,6,32,128]{3,2,0,1:T(8,128)S(1)} %constant_dynamic-slice_fusion.9), channel_id=1, source_target_pairs={{0,2},{1,3},{2,4},{3,5},{4,6},{5,7},{6,0},{7,1},{8,10},{9,11},{10,... | collective-permute-start | bytes 1179656 | tf_op jit(solution)/shard_map/ppermute | solution.py:12
  143.0 17.7 %collective-permute-start.7 = (f32[4,6,32,128]{3,2,0,1:T(8,128)S(1)}, f32[4,6,32,128]{3,2,0,1:T(8,128)S(1)}, u32[]{:S(2)}, u32[]{:S(2)}) collective-permute-start(f32[4,6,32,128]{3,2,0,1:T(8,128)S(1)} %dynamic-slice_add_fusion.14), channel_id=1, source_target_pairs={{0,6},{1,7},{2,0},{3,1},{4,2},{5,3},{6,4},{7,5},{8,14},{9,15},{10,... | collective-permute-start | bytes 1179656 | tf_op jit(solution)/shard_map/ppermute | solution.py:12
  146.3 18.2 %collective-permute-start.4 = (f32[4,6,32,128]{3,2,0,1:T(8,128)S(1)}, f32[4,6,32,128]{3,2,0,1:T(8,128)S(1)}, u32[]{:S(2)}, u32[]{:S(2)}) collective-permute-start(f32[4,6,32,128]{3,2,0,1:T(8,128)S(1)} %dynamic-slice_add_fusion.17), channel_id=1, source_target_pairs={{0,2},{1,3},{2,4},{3,5},{4,6},{5,7},{6,0},{7,1},{8,10},{9,11},{10,... | collective-permute-start | bytes 1179656 | tf_op jit(solution)/shard_map/ppermute | solution.py:12
  146.5 22.6 %collective-permute-start.14 = (f32[4,6,32,128]{3,2,0,1:T(8,128)S(1)}, f32[4,6,32,128]{3,2,0,1:T(8,128)S(1)}, u32[]{:S(2)}, u32[]{:S(2)}) collective-permute-start(f32[4,6,32,128]{3,2,0,1:T(8,128)S(1)} %dynamic-slice_add_fusion.8), channel_id=1, source_target_pairs={{0,6},{1,7},{2,0},{3,1},{4,2},{5,3},{6,4},{7,5},{8,14},{9,15},{10,... | collective-permute-start | bytes 1179656 | tf_op jit(solution)/shard_map/ppermute | solution.py:12
  152.3 20.7 %collective-permute-start.11 = (f32[4,6,32,128]{3,2,0,1:T(8,128)S(1)}, f32[4,6,32,128]{3,2,0,1:T(8,128)S(1)}, u32[]{:S(2)}, u32[]{:S(2)}) collective-permute-start(f32[4,6,32,128]{3,2,0,1:T(8,128)S(1)} %dynamic-slice_add_fusion.11), channel_id=1, source_target_pairs={{0,2},{1,3},{2,4},{3,5},{4,6},{5,7},{6,0},{7,1},{8,10},{9,11},{10,... | collective-permute-start | bytes 1179656 | tf_op jit(solution)/shard_map/ppermute | solution.py:12
  156.1 21.5 %collective-permute-start.21 = (f32[4,6,32,128]{3,2,0,1:T(8,128)S(1)}, f32[4,6,32,128]{3,2,0,1:T(8,128)S(1)}, u32[]{:S(2)}, u32[]{:S(2)}) collective-permute-start(f32[4,6,32,128]{3,2,0,1:T(8,128)S(1)} %dynamic-slice_add_fusion.2), channel_id=1, source_target_pairs={{0,6},{1,7},{2,0},{3,1},{4,2},{5,3},{6,4},{7,5},{8,14},{9,15},{10,... | collective-permute-start | bytes 1179656 | tf_op jit(solution)/shard_map/ppermute | solution.py:12
  160.7 20.7 %collective-permute-start.18 = (f32[4,6,32,128]{3,2,0,1:T(8,128)S(1)}, f32[4,6,32,128]{3,2,0,1:T(8,128)S(1)}, u32[]{:S(2)}, u32[]{:S(2)}) collective-permute-start(f32[4,6,32,128]{3,2,0,1:T(8,128)S(1)} %dynamic-slice_add_fusion.5), channel_id=1, source_target_pairs={{0,2},{1,3},{2,4},{3,5},{4,6},{5,7},{6,0},{7,1},{8,10},{9,11},{10,... | collective-permute-start | bytes 1179656 | tf_op jit(solution)/shard_map/ppermute | solution.py:12
  164.5 21.5 %collective-permute-start.8 = (f32[4,6,32,128]{3,2,0,1:T(8,128)S(1)}, f32[4,6,32,128]{3,2,0,1:T(8,128)S(1)}, u32[]{:S(2)}, u32[]{:S(2)}) collective-permute-start(f32[4,6,32,128]{3,2,0,1:T(8,128)S(1)} %dynamic-slice_add_fusion.13), channel_id=1, source_target_pairs={{0,6},{1,7},{2,0},{3,1},{4,2},{5,3},{6,4},{7,5},{8,14},{9,15},{10,... | collective-permute-start | bytes 1179656 | tf_op jit(solution)/shard_map/ppermute | solution.py:12
  169.1 20.7 %collective-permute-start.5 = (f32[4,6,32,128]{3,2,0,1:T(8,128)S(1)}, f32[4,6,32,128]{3,2,0,1:T(8,128)S(1)}, u32[]{:S(2)}, u32[]{:S(2)}) collective-permute-start(f32[4,6,32,128]{3,2,0,1:T(8,128)S(1)} %dynamic-slice_add_fusion.16), channel_id=1, source_target_pairs={{0,2},{1,3},{2,4},{3,5},{4,6},{5,7},{6,0},{7,1},{8,10},{9,11},{10,... | collective-permute-start | bytes 1179656 | tf_op jit(solution)/shard_map/ppermute | solution.py:12
  172.9 21.5 %collective-permute-start.15 = (f32[4,6,32,128]{3,2,0,1:T(8,128)S(1)}, f32[4,6,32,128]{3,2,0,1:T(8,128)S(1)}, u32[]{:S(2)}, u32[]{:S(2)}) collective-permute-start(f32[4,6,32,128]{3,2,0,1:T(8,128)S(1)} %dynamic-slice_add_fusion.7), channel_id=1, source_target_pairs={{0,6},{1,7},{2,0},{3,1},{4,2},{5,3},{6,4},{7,5},{8,14},{9,15},{10,... | collective-permute-start | bytes 1179656 | tf_op jit(solution)/shard_map/ppermute | solution.py:12
  177.5 20.7 %collective-permute-start.12 = (f32[4,6,32,128]{3,2,0,1:T(8,128)S(1)}, f32[4,6,32,128]{3,2,0,1:T(8,128)S(1)}, u32[]{:S(2)}, u32[]{:S(2)}) collective-permute-start(f32[4,6,32,128]{3,2,0,1:T(8,128)S(1)} %dynamic-slice_add_fusion.10), channel_id=1, source_target_pairs={{0,2},{1,3},{2,4},{3,5},{4,6},{5,7},{6,0},{7,1},{8,10},{9,11},{10,... | collective-permute-start | bytes 1179656 | tf_op jit(solution)/shard_map/ppermute | solution.py:12
  181.3 20.2 %collective-permute-start.22 = (f32[4,6,32,128]{3,2,0,1:T(8,128)S(1)}, f32[4,6,32,128]{3,2,0,1:T(8,128)S(1)}, u32[]{:S(2)}, u32[]{:S(2)}) collective-permute-start(f32[4,6,32,128]{3,2,0,1:T(8,128)S(1)} %dynamic-slice_add_fusion.1), channel_id=1, source_target_pairs={{0,6},{1,7},{2,0},{3,1},{4,2},{5,3},{6,4},{7,5},{8,14},{9,15},{10,... | collective-permute-start | bytes 1179656 | tf_op jit(solution)/shard_map/ppermute | solution.py:12
  186.0 18.0 %collective-permute-start.19 = (f32[4,6,32,128]{3,2,0,1:T(8,128)S(1)}, f32[4,6,32,128]{3,2,0,1:T(8,128)S(1)}, u32[]{:S(2)}, u32[]{:S(2)}) collective-permute-start(f32[4,6,32,128]{3,2,0,1:T(8,128)S(1)} %dynamic-slice_add_fusion.4), channel_id=1, source_target_pairs={{0,2},{1,3},{2,4},{3,5},{4,6},{5,7},{6,0},{7,1},{8,10},{9,11},{10,... | collective-permute-start | bytes 1179656 | tf_op jit(solution)/shard_map/ppermute | solution.py:12
  189.9 17.4 %collective-permute-start.9 = (f32[4,12,16,128]{3,2,0,1:T(8,128)S(1)}, f32[4,12,16,128]{3,2,0,1:T(8,128)S(1)}, u32[]{:S(2)}, u32[]{:S(2)}) collective-permute-start(f32[4,12,16,128]{3,2,0,1:T(8,128)S(1)} %fusion.21), channel_id=1, source_target_pairs={{0,1},{1,0},{2,3},{3,2},{4,5},{5,4},{6,7},{7,6},{8,9},{9,8},{10,11... | collective-permute-start | bytes 1179656 | tf_op jit(solution)/shard_map/ppermute | solution.py:12
  198.3 11.4 %collective-permute-start.16 = (f32[4,12,16,128]{3,2,0,1:T(8,128)S(1)}, f32[4,12,16,128]{3,2,0,1:T(8,128)S(1)}, u32[]{:S(2)}, u32[]{:S(2)}) collective-permute-start(f32[4,12,16,128]{3,2,0,1:T(8,128)S(1)} %fusion.18), channel_id=1, source_target_pairs={{0,1},{1,0},{2,3},{3,2},{4,5},{5,4},{6,7},{7,6},{8,9},{9,8},{10,11... | collective-permute-start | bytes 1179656 | tf_op jit(solution)/shard_map/ppermute | solution.py:12
  204.0 12.1 %collective-permute-start.23 = (f32[4,12,16,128]{3,2,0,1:T(8,128)S(1)}, f32[4,12,16,128]{3,2,0,1:T(8,128)S(1)}, u32[]{:S(2)}, u32[]{:S(2)}) collective-permute-start(f32[4,12,16,128]{3,2,0,1:T(8,128)S(1)} %fusion.15), channel_id=1, source_target_pairs={{0,1},{1,0},{2,3},{3,2},{4,5},{5,4},{6,7},{7,6},{8,9},{9,8},{10,11... | collective-permute-start | bytes 1179656 | tf_op jit(solution)/shard_map/ppermute | solution.py:12
  238.4 14.4 %collective-permute-start.25 = (f32[1,144,256]{2,1,0:T(8,128)S(1)}, f32[1,144,256]{2,1,0:T(8,128)S(1)}, u32[]{:S(2)}, u32[]{:S(2)}) collective-permute-start(f32[1,144,256]{2,1,0:T(8,128)S(1)} %get-tuple-element.17), channel_id=1, source_target_pairs={{0,1},{1,0},{2,3},{3,2},{4,5},{5,4},{6,7},{7,6},{8,33},{9,32},{10,... | collective-permute-start | bytes 442376 | tf_op jit(solution)/shard_map/ppermute | solution.py:101
  241.7 11.2 %collective-permute-start.26 = (f32[1,144,256]{2,1,0:T(8,128)S(1)}, f32[1,144,256]{2,1,0:T(8,128)S(1)}, u32[]{:S(2)}, u32[]{:S(2)}) collective-permute-start(f32[1,144,256]{2,1,0:T(8,128)S(1)} %get-tuple-element.16), channel_id=1, source_target_pairs={{0,2},{1,3},{2,0},{3,1},{4,6},{5,7},{6,4},{7,5},{8,34},{9,35},{10,... | collective-permute-start | bytes 442376 | tf_op jit(solution)/shard_map/ppermute | solution.py:101
  241.7 22.7 %collective-permute-start.27 = (f32[1,144,256]{2,1,0:T(8,128)S(1)}, f32[1,144,256]{2,1,0:T(8,128)S(1)}, u32[]{:S(2)}, u32[]{:S(2)}) collective-permute-start(f32[1,144,256]{2,1,0:T(8,128)S(1)} %get-tuple-element.15), channel_id=1, source_target_pairs={{0,3},{1,2},{2,1},{3,0},{4,7},{5,6},{6,5},{7,4},{8,35},{9,34},{10,... | collective-permute-start | bytes 442376 | tf_op jit(solution)/shard_map/ppermute | solution.py:101
  243.5 20.9 %collective-permute-start.28 = (f32[1,144,256]{2,1,0:T(8,128)S(1)}, f32[1,144,256]{2,1,0:T(8,128)S(1)}, u32[]{:S(2)}, u32[]{:S(2)}) collective-permute-start(f32[1,144,256]{2,1,0:T(8,128)S(1)} %get-tuple-element.14), channel_id=1, source_target_pairs={{0,4},{1,5},{2,6},{3,7},{4,0},{5,1},{6,2},{7,3},{8,36},{9,37},{10,... | collective-permute-start | bytes 442376 | tf_op jit(solution)/shard_map/ppermute | solution.py:101
  244.9 36.2 %collective-permute-start.29 = (f32[1,144,256]{2,1,0:T(8,128)S(1)}, f32[1,144,256]{2,1,0:T(8,128)S(1)}, u32[]{:S(2)}, u32[]{:S(2)}) collective-permute-start(f32[1,144,256]{2,1,0:T(8,128)S(1)} %get-tuple-element.13), channel_id=1, source_target_pairs={{0,5},{1,4},{2,7},{3,6},{4,1},{5,0},{6,3},{7,2},{8,37},{9,36},{10,... | collective-permute-start | bytes 442376 | tf_op jit(solution)/shard_map/ppermute | solution.py:101
  252.8 28.3 %collective-permute-start.30 = (f32[1,144,256]{2,1,0:T(8,128)S(1)}, f32[1,144,256]{2,1,0:T(8,128)S(1)}, u32[]{:S(2)}, u32[]{:S(2)}) collective-permute-start(f32[1,144,256]{2,1,0:T(8,128)S(1)} %get-tuple-element.12), channel_id=1, source_target_pairs={{0,6},{1,7},{2,4},{3,5},{4,2},{5,3},{6,0},{7,1},{8,38},{9,39},{10,... | collective-permute-start | bytes 442376 | tf_op jit(solution)/shard_map/ppermute | solution.py:101
  252.9 31.1 %collective-permute-start.31 = (f32[1,144,256]{2,1,0:T(8,128)S(1)}, f32[1,144,256]{2,1,0:T(8,128)S(1)}, u32[]{:S(2)}, u32[]{:S(2)}) collective-permute-start(f32[1,144,256]{2,1,0:T(8,128)S(1)} %get-tuple-element.11), channel_id=1, source_target_pairs={{0,7},{1,6},{2,5},{3,4},{4,3},{5,2},{6,1},{7,0},{8,39},{9,38},{10,... | collective-permute-start | bytes 442376 | tf_op jit(solution)/shard_map/ppermute | solution.py:101
  (4 other events, 37.3 us)
Sparse Core Ops, SparseCore 0:
  10.2 96.0 all-gather.1
